TPU v7x, 32 devices: a whole 2x2x4 slice. The times are simulated.
32 devices in a mesh: section: 4 (over x, core), expert: 8 (over z, y).
Axes of the slice: x: 2, y: 2, z: 4, core: 2. Of those that a mesh axis runs over, the one named last changes fastest.
Arguments:
- layer_inputs: bfloat16 [4, 8, 128, 2048], P('section', None, 'expert'), may hold values from -6 to 6
- top_grad: bfloat16 [8, 128, 2048], P('section', 'expert'), may hold values from -6 to 6
- expert_ids: int32 [4, 8, 128, 4], P('section', None, 'expert'), may hold values from 0 to 7, all different within a row; in each aligned block of 16 rows (0 to 15, 16 to 31, ..., all dimensions but the last counted through in order) at most 9 rows name the same one
- router: bfloat16 [4, 2048, 8], P('section'), may hold values from -0.125 to 0.125
- norm_gain: bfloat16 [4, 2048], P('section'), may hold values from 0.099609375 to 1.8984375
- w_gate: bfloat16 [4, 8, 2048, 1024], P('section', 'expert'), may hold values from -0.125 to 0.125
- w_up: bfloat16 [4, 8, 2048, 1024], P('section', 'expert'), may hold values from -0.125 to 0.125
- w_down: bfloat16 [4, 8, 1024, 2048], P('section', 'expert'), may hold values from -0.1875 to 0.1875
Outputs:
- input_grads: bfloat16 [4, 8, 128, 2048], P('section', None, 'expert')
Inputs may be any that keep to these rules, and one draw needn't show every extreme that they name: `expert_ids`: each token names 4 different experts. Among the 16 tokens of one device in one micro-batch of one layer, no expert is named by more than 9 of them, and in some of these blocks one expert is named by exactly 9.
All inputs are finite; a program needn't handle non-finite values.
Results may differ from a plain program's by a relative error of at most 0.015.
Values may be sent and summed in bfloat16 or wider, within the bound.
No kernel may reach another device: no remote copies, remote signals or barrier semaphores. Data moves between devices by JAX's collectives and lax.ppermute only.
A program may use at most 128 MiB of HBM per device.

v0:
```python
import jax
import jax.numpy as jnp
from jax import lax
from jax.sharding import PartitionSpec as P


def shifted(shard, axis, by):
    devices = lax.axis_size(axis)
    pairs = [(i, i + by) for i in range(devices) if 0 <= i + by < devices]
    return lax.ppermute(shard, axis, pairs)


def prepare(x_rows, gain):
    x_float = x_rows.astype(jnp.float32)
    inverse = lax.rsqrt(jnp.mean(x_float * x_float, axis=-1, keepdims=True) + 1e-05)
    normed = (x_float * inverse * gain).astype(jnp.bfloat16)
    return (x_float, inverse, normed)


def expert_rows(normed_rows, grad_rows, gate_w, up_w, down_w):
    gate = jnp.dot(normed_rows, gate_w, preferred_element_type=jnp.float32)
    up_rows = jnp.dot(normed_rows, up_w, preferred_element_type=jnp.float32)
    squash = jax.nn.sigmoid(gate)
    active = gate * squash
    hidden = (active * up_rows).astype(jnp.bfloat16)
    output = jnp.dot(hidden, down_w, preferred_element_type=jnp.float32)
    dprob = jnp.sum(output * grad_rows.astype(jnp.float32), axis=-1)
    dhidden = lax.dot_general(
        grad_rows, down_w, (((1,), (1,)), ((), ())), preferred_element_type=jnp.float32
    )
    dgate = (dhidden * up_rows * squash * (1.0 + gate * (1.0 - squash))).astype(jnp.bfloat16)
    dup = (dhidden * active).astype(jnp.bfloat16)
    returned = lax.dot_general(
        dgate, gate_w, (((1,), (1,)), ((), ())), preferred_element_type=jnp.float32
    )
    returned = returned + lax.dot_general(
        dup, up_w, (((1,), (1,)), ((), ())), preferred_element_type=jnp.float32
    )
    return (returned.astype(jnp.bfloat16), dprob)


def finish(x_float, inverse, normed, gain, router_layer, ids, grad_in, pair_back, pair_prob):
    logits = jnp.dot(normed, router_layer, preferred_element_type=jnp.float32)
    raised = jnp.exp(logits)
    probs = raised / jnp.sum(raised, axis=-1, keepdims=True)
    choose = (ids[..., None] == jnp.arange(router_layer.shape[1], dtype=jnp.int32)).astype(
        jnp.float32
    )
    picked = jnp.sum(probs[..., None, :] * choose, axis=-1)
    dfull = jnp.sum(pair_prob[..., None] * choose, axis=-2)
    dlogit = probs * (dfull - jnp.sum(probs * dfull, axis=-1, keepdims=True))
    router_term = jnp.dot(
        dlogit, router_layer.astype(jnp.float32).T, precision=lax.Precision.HIGHEST
    )
    dnormed = jnp.sum(picked[..., None] * pair_back, axis=-2) + router_term
    scaled = gain * dnormed
    inner = jnp.mean(x_float * scaled, axis=-1, keepdims=True)
    result = (
        grad_in.astype(jnp.float32)
        + inverse * scaled
        - x_float * inverse * inverse * inverse * inner
    )
    return result.astype(jnp.bfloat16)


def selection(ids, experts, capacity):
    pair_ids = ids.reshape(-1)
    onehot = (pair_ids[:, None] == jnp.arange(experts, dtype=jnp.int32)[None, :]).astype(jnp.int32)
    ranks = jnp.sum(onehot * (jnp.cumsum(onehot, axis=0) - 1), axis=1)
    target = pair_ids * capacity + ranks
    return (target[:, None] == jnp.arange(experts * capacity, dtype=jnp.int32)[None, :]).astype(
        jnp.bfloat16
    )


def pack_rows(select, rows, per_token):
    repeated = jnp.repeat(rows, per_token, axis=0)
    packed = lax.dot_general(
        select, repeated, (((0,), (0,)), ((), ())), preferred_element_type=jnp.float32
    )
    return packed.astype(jnp.bfloat16)


def pick_micro(values, index):
    return lax.dynamic_index_in_dim(values, index, 0, False)


def shards(layer_inputs, top_grad, expert_ids, router, norm_gain, w_gate, w_up, w_down):
    segments = lax.axis_size("section")
    experts = lax.axis_size("expert")
    segment_index = lax.axis_index("section")
    micro = layer_inputs.shape[1]
    tok_rows = layer_inputs.shape[2]
    width = layer_inputs.shape[3]
    per_token = expert_ids.shape[3]
    capacity = min(tok_rows, per_token * tok_rows // experts + max(1, tok_rows // 16))
    slots = experts * capacity
    gain = norm_gain[0].astype(jnp.float32)
    router_layer = router[0]
    gate_layer = w_gate[0, 0]
    up_layer = w_up[0, 0]
    down_layer = w_down[0, 0]
    ids_layer = expert_ids[0]
    x_layer = layer_inputs[0]
    top_full = lax.all_gather(top_grad, "section", axis=0, tiled=True)

    def advance(step, carry):
        previous, collected = carry
        arrived = shifted(previous, "section", -1)
        position = step - (segments - 1 - segment_index)
        working = jnp.logical_and(position >= 0, position < micro)
        chosen = jnp.clip(position, 0, micro - 1)
        grad_in = jnp.where(segment_index == segments - 1, pick_micro(top_full, chosen), arrived)
        ids_now = pick_micro(ids_layer, chosen)
        select = selection(ids_now, experts, capacity)
        x_float, inverse, normed = prepare(pick_micro(x_layer, chosen), gain)
        sent_normed = pack_rows(select, normed, per_token).reshape(experts, capacity, width)
        sent_grad = pack_rows(select, grad_in, per_token).reshape(experts, capacity, width)
        got_normed, got_grad = (
            lax.all_to_all(sent_normed, "expert", split_axis=0, concat_axis=0, tiled=True),
            lax.all_to_all(sent_grad, "expert", split_axis=0, concat_axis=0, tiled=True),
        )
        rows_normed = got_normed.reshape(slots, width)
        rows_grad = got_grad.reshape(slots, width)

        def run_expert(operands):
            return expert_rows(operands[0], operands[1], gate_layer, up_layer, down_layer)

        def skip_expert(operands):
            return (jnp.zeros((slots, width), jnp.bfloat16), jnp.zeros((slots,), jnp.float32))

        returned, dprob = lax.cond(working, run_expert, skip_expert, (rows_normed, rows_grad))
        back_home, prob_home = (
            lax.all_to_all(
                returned.reshape(experts, capacity, width),
                "expert",
                split_axis=0,
                concat_axis=0,
                tiled=True,
            ),
            lax.all_to_all(
                dprob.reshape(experts, capacity).astype(jnp.bfloat16),
                "expert",
                split_axis=0,
                concat_axis=0,
                tiled=True,
            ).astype(jnp.float32),
        )
        pair_back = lax.dot_general(
            select,
            back_home.reshape(slots, width),
            (((1,), (0,)), ((), ())),
            preferred_element_type=jnp.float32,
        )
        pair_back = pair_back.reshape(tok_rows, per_token, width)
        pair_prob = jnp.dot(
            select.astype(jnp.float32), prob_home.reshape(slots), precision=lax.Precision.HIGHEST
        )
        pair_prob = pair_prob.reshape(tok_rows, per_token)
        result = finish(
            x_float, inverse, normed, gain, router_layer, ids_now, grad_in, pair_back, pair_prob
        )
        retained = pick_micro(collected, chosen)
        collected = lax.dynamic_update_index_in_dim(
            collected, jnp.where(working, result, retained), chosen, 0
        )
        return (result, collected)

    start = (
        jnp.zeros((tok_rows, width), jnp.bfloat16),
        jnp.zeros((micro, tok_rows, width), jnp.bfloat16),
    )
    final_grad, collected = lax.fori_loop(0, micro + segments - 1, advance, start)
    return collected.reshape(1, micro, tok_rows, width)


def solution(mesh):
    placed = (
        P("section", None, "expert", None),
        P("section", "expert", None),
        P("section", None, "expert", None),
        P("section", None, None),
        P("section", None),
        P("section", "expert", None, None),
        P("section", "expert", None, None),
        P("section", "expert", None, None),
    )
    return jax.shard_map(
        shards,
        mesh=mesh,
        in_specs=placed,
        out_specs=P("section", None, "expert", None),
        check_vma=False,
    )
```

profile of v0, /device:TPU:2, one launch (start us, length us, event | category | flops | bytes accessed | tf_op | source)
XLA Modules:
  0.0 932.1 jit_solution(10642153080023947241)
XLA Ops:
  9.2 922.1 %while.18 = (s32[]{:T(128)}, bf16[16,2048]{1,0:T(8,128)(2,1)S(1)}, bf16[8,16,2048]{2,1,0:T(8,128)(2,1)S(1)}, pred[]{:T(512)}, s32[]{:T(128)}, /*index=5*/bf16[8,...) while((s32[]{:T(128)}, bf16[16,2048]{1,0:T(8,128)(2,1)S(1)}, ...), condition=%wide.region_13.14_spmd.clone, body=%wide.region_0.13_spmd.clone.sunk | while | flops 1876001664 | bytes 93928576 | solution.py:173
  40.5 14.4 %all-to-all-done = bf16[8,9,2048]{2,1,0:T(8,128)(2,1)S(1)} async-done(((bf16[8,9,2048]{2,1,0:T(8,128)(2,1)}), bf16[8,9,2048]{2,1,0:T(8,128)(2,1)S(1)}, u32[]{:S(2)}, u32[]{:S(2)}) %all-to-all-start) | async-done | bytes 294944 | tf_op jit(solution)/shard_map/while/body/eval_jaxpr/all_to_all | solution.py:121
  120.1 14.1 %conditional.3 = (bf16[72,2048]{1,0:T(8,128)(2,1)S(1)}, bf16[72]{0:T(256)(128)(2,1)S(1)}) conditional(s32[]{:T(128)} %convert_element_type.180, () %tuple.64, (bf16[8,9,2048]{2,1,0:T(8,128)(2,1)S(1)}, bf16[1024,2048]{1,0:T(8,128)(2,1)}, bf16[8,9,2048]{2,1,0:T(8,128)(2,1)S(1)}, bf16[2048,1024]{1,0:T(8,128)(2,1)}, bf16[2048,1024]{1,0:T(8,128)(2,1)}) %tuple.65), branch_computations={%region_6.6_spmd, %region_7.8_spmd} | conditional | flops 1814298624 | bytes 82280696 | solution.py:132
  151.3 14.9 %all-to-all-done.2 = bf16[8,9,2048]{2,1,0:T(8,128)(2,1)S(1)} async-done(((bf16[8,9,2048]{2,1,0:T(8,128)(2,1)}), bf16[8,9,2048]{2,1,0:T(8,128)(2,1)S(1)}, u32[]{:S(2)}, u32[]{:S(2)}) %all-to-all-start.2) | async-done | bytes 294944 | tf_op jit(solution)/shard_map/while/body/eval_jaxpr/all_to_all | solution.py:134
  180.9 13.7 %all-to-all-done.1 = bf16[8,9,2048]{2,1,0:T(8,128)(2,1)S(1)} async-done(((bf16[8,9,2048]{2,1,0:T(8,128)(2,1)}), bf16[8,9,2048]{2,1,0:T(8,128)(2,1)S(1)}, u32[]{:S(2)}, u32[]{:S(2)}) %all-to-all-start.1) | async-done | bytes 294944 | tf_op jit(solution)/shard_map/while/body/eval_jaxpr/all_to_all | solution.py:120
  198.4 14.5 %all-to-all-done = bf16[8,9,2048]{2,1,0:T(8,128)(2,1)S(1)} async-done(((bf16[8,9,2048]{2,1,0:T(8,128)(2,1)}), bf16[8,9,2048]{2,1,0:T(8,128)(2,1)S(1)}, u32[]{:S(2)}, u32[]{:S(2)}) %all-to-all-start) | async-done | bytes 294944 | tf_op jit(solution)/shard_map/while/body/eval_jaxpr/all_to_all | solution.py:121
  212.9 14.1 %conditional.3 = (bf16[72,2048]{1,0:T(8,128)(2,1)S(1)}, bf16[72]{0:T(256)(128)(2,1)S(1)}) conditional(s32[]{:T(128)} %convert_element_type.180, () %tuple.64, (bf16[8,9,2048]{2,1,0:T(8,128)(2,1)S(1)}, bf16[1024,2048]{1,0:T(8,128)(2,1)}, bf16[8,9,2048]{2,1,0:T(8,128)(2,1)S(1)}, bf16[2048,1024]{1,0:T(8,128)(2,1)}, bf16[2048,1024]{1,0:T(8,128)(2,1)}) %tuple.65), branch_computations={%region_6.6_spmd, %region_7.8_spmd} | conditional | flops 1814298624 | bytes 82280696 | solution.py:132
  269.0 13.7 %all-to-all-done.1 = bf16[8,9,2048]{2,1,0:T(8,128)(2,1)S(1)} async-done(((bf16[8,9,2048]{2,1,0:T(8,128)(2,1)}), bf16[8,9,2048]{2,1,0:T(8,128)(2,1)S(1)}, u32[]{:S(2)}, u32[]{:S(2)}) %all-to-all-start.1) | async-done | bytes 294944 | tf_op jit(solution)/shard_map/while/body/eval_jaxpr/all_to_all | solution.py:120
  286.6 14.5 %all-to-all-done = bf16[8,9,2048]{2,1,0:T(8,128)(2,1)S(1)} async-done(((bf16[8,9,2048]{2,1,0:T(8,128)(2,1)}), bf16[8,9,2048]{2,1,0:T(8,128)(2,1)S(1)}, u32[]{:S(2)}, u32[]{:S(2)}) %all-to-all-start) | async-done | bytes 294944 | tf_op jit(solution)/shard_map/while/body/eval_jaxpr/all_to_all | solution.py:121
  301.1 14.1 %conditional.3 = (bf16[72,2048]{1,0:T(8,128)(2,1)S(1)}, bf16[72]{0:T(256)(128)(2,1)S(1)}) conditional(s32[]{:T(128)} %convert_element_type.180, () %tuple.64, (bf16[8,9,2048]{2,1,0:T(8,128)(2,1)S(1)}, bf16[1024,2048]{1,0:T(8,128)(2,1)}, bf16[8,9,2048]{2,1,0:T(8,128)(2,1)S(1)}, bf16[2048,1024]{1,0:T(8,128)(2,1)}, bf16[2048,1024]{1,0:T(8,128)(2,1)}) %tuple.65), branch_computations={%region_6.6_spmd, %region_7.8_spmd} | conditional | flops 1814298624 | bytes 82280696 | solution.py:132
  329.9 13.0 %all-to-all-done.2 = bf16[8,9,2048]{2,1,0:T(8,128)(2,1)S(1)} async-done(((bf16[8,9,2048]{2,1,0:T(8,128)(2,1)}), bf16[8,9,2048]{2,1,0:T(8,128)(2,1)S(1)}, u32[]{:S(2)}, u32[]{:S(2)}) %all-to-all-start.2) | async-done | bytes 294944 | tf_op jit(solution)/shard_map/while/body/eval_jaxpr/all_to_all | solution.py:134
  357.2 13.7 %all-to-all-done.1 = bf16[8,9,2048]{2,1,0:T(8,128)(2,1)S(1)} async-done(((bf16[8,9,2048]{2,1,0:T(8,128)(2,1)}), bf16[8,9,2048]{2,1,0:T(8,128)(2,1)S(1)}, u32[]{:S(2)}, u32[]{:S(2)}) %all-to-all-start.1) | async-done | bytes 294944 | tf_op jit(solution)/shard_map/while/body/eval_jaxpr/all_to_all | solution.py:120
  374.7 14.5 %all-to-all-done = bf16[8,9,2048]{2,1,0:T(8,128)(2,1)S(1)} async-done(((bf16[8,9,2048]{2,1,0:T(8,128)(2,1)}), bf16[8,9,2048]{2,1,0:T(8,128)(2,1)S(1)}, u32[]{:S(2)}, u32[]{:S(2)}) %all-to-all-start) | async-done | bytes 294944 | tf_op jit(solution)/shard_map/while/body/eval_jaxpr/all_to_all | solution.py:121
  389.2 14.1 %conditional.3 = (bf16[72,2048]{1,0:T(8,128)(2,1)S(1)}, bf16[72]{0:T(256)(128)(2,1)S(1)}) conditional(s32[]{:T(128)} %convert_element_type.180, () %tuple.64, (bf16[8,9,2048]{2,1,0:T(8,128)(2,1)S(1)}, bf16[1024,2048]{1,0:T(8,128)(2,1)}, bf16[8,9,2048]{2,1,0:T(8,128)(2,1)S(1)}, bf16[2048,1024]{1,0:T(8,128)(2,1)}, bf16[2048,1024]{1,0:T(8,128)(2,1)}) %tuple.65), branch_computations={%region_6.6_spmd, %region_7.8_spmd} | conditional | flops 1814298624 | bytes 82280696 | solution.py:132
  445.4 13.7 %all-to-all-done.1 = bf16[8,9,2048]{2,1,0:T(8,128)(2,1)S(1)} async-done(((bf16[8,9,2048]{2,1,0:T(8,128)(2,1)}), bf16[8,9,2048]{2,1,0:T(8,128)(2,1)S(1)}, u32[]{:S(2)}, u32[]{:S(2)}) %all-to-all-start.1) | async-done | bytes 294944 | tf_op jit(solution)/shard_map/while/body/eval_jaxpr/all_to_all | solution.py:120
  462.9 14.5 %all-to-all-done = bf16[8,9,2048]{2,1,0:T(8,128)(2,1)S(1)} async-done(((bf16[8,9,2048]{2,1,0:T(8,128)(2,1)}), bf16[8,9,2048]{2,1,0:T(8,128)(2,1)S(1)}, u32[]{:S(2)}, u32[]{:S(2)}) %all-to-all-start) | async-done | bytes 294944 | tf_op jit(solution)/shard_map/while/body/eval_jaxpr/all_to_all | solution.py:121
  477.4 14.1 %conditional.3 = (bf16[72,2048]{1,0:T(8,128)(2,1)S(1)}, bf16[72]{0:T(256)(128)(2,1)S(1)}) conditional(s32[]{:T(128)} %convert_element_type.180, () %tuple.64, (bf16[8,9,2048]{2,1,0:T(8,128)(2,1)S(1)}, bf16[1024,2048]{1,0:T(8,128)(2,1)}, bf16[8,9,2048]{2,1,0:T(8,128)(2,1)S(1)}, bf16[2048,1024]{1,0:T(8,128)(2,1)}, bf16[2048,1024]{1,0:T(8,128)(2,1)}) %tuple.65), branch_computations={%region_6.6_spmd, %region_7.8_spmd} | conditional | flops 1814298624 | bytes 82280696 | solution.py:132
  533.5 13.7 %all-to-all-done.1 = bf16[8,9,2048]{2,1,0:T(8,128)(2,1)S(1)} async-done(((bf16[8,9,2048]{2,1,0:T(8,128)(2,1)}), bf16[8,9,2048]{2,1,0:T(8,128)(2,1)S(1)}, u32[]{:S(2)}, u32[]{:S(2)}) %all-to-all-start.1) | async-done | bytes 294944 | tf_op jit(solution)/shard_map/while/body/eval_jaxpr/all_to_all | solution.py:120
  551.0 14.5 %all-to-all-done = bf16[8,9,2048]{2,1,0:T(8,128)(2,1)S(1)} async-done(((bf16[8,9,2048]{2,1,0:T(8,128)(2,1)}), bf16[8,9,2048]{2,1,0:T(8,128)(2,1)S(1)}, u32[]{:S(2)}, u32[]{:S(2)}) %all-to-all-start) | async-done | bytes 294944 | tf_op jit(solution)/shard_map/while/body/eval_jaxpr/all_to_all | solution.py:121
  565.5 14.1 %conditional.3 = (bf16[72,2048]{1,0:T(8,128)(2,1)S(1)}, bf16[72]{0:T(256)(128)(2,1)S(1)}) conditional(s32[]{:T(128)} %convert_element_type.180, () %tuple.64, (bf16[8,9,2048]{2,1,0:T(8,128)(2,1)S(1)}, bf16[1024,2048]{1,0:T(8,128)(2,1)}, bf16[8,9,2048]{2,1,0:T(8,128)(2,1)S(1)}, bf16[2048,1024]{1,0:T(8,128)(2,1)}, bf16[2048,1024]{1,0:T(8,128)(2,1)}) %tuple.65), branch_computations={%region_6.6_spmd, %region_7.8_spmd} | conditional | flops 1814298624 | bytes 82280696 | solution.py:132
  621.7 13.7 %all-to-all-done.1 = bf16[8,9,2048]{2,1,0:T(8,128)(2,1)S(1)} async-done(((bf16[8,9,2048]{2,1,0:T(8,128)(2,1)}), bf16[8,9,2048]{2,1,0:T(8,128)(2,1)S(1)}, u32[]{:S(2)}, u32[]{:S(2)}) %all-to-all-start.1) | async-done | bytes 294944 | tf_op jit(solution)/shard_map/while/body/eval_jaxpr/all_to_all | solution.py:120
  639.2 14.5 %all-to-all-done = bf16[8,9,2048]{2,1,0:T(8,128)(2,1)S(1)} async-done(((bf16[8,9,2048]{2,1,0:T(8,128)(2,1)}), bf16[8,9,2048]{2,1,0:T(8,128)(2,1)S(1)}, u32[]{:S(2)}, u32[]{:S(2)}) %all-to-all-start) | async-done | bytes 294944 | tf_op jit(solution)/shard_map/while/body/eval_jaxpr/all_to_all | solution.py:121
  653.7 14.1 %conditional.3 = (bf16[72,2048]{1,0:T(8,128)(2,1)S(1)}, bf16[72]{0:T(256)(128)(2,1)S(1)}) conditional(s32[]{:T(128)} %convert_element_type.180, () %tuple.64, (bf16[8,9,2048]{2,1,0:T(8,128)(2,1)S(1)}, bf16[1024,2048]{1,0:T(8,128)(2,1)}, bf16[8,9,2048]{2,1,0:T(8,128)(2,1)S(1)}, bf16[2048,1024]{1,0:T(8,128)(2,1)}, bf16[2048,1024]{1,0:T(8,128)(2,1)}) %tuple.65), branch_computations={%region_6.6_spmd, %region_7.8_spmd} | conditional | flops 1814298624 | bytes 82280696 | solution.py:132
  709.8 13.7 %all-to-all-done.1 = bf16[8,9,2048]{2,1,0:T(8,128)(2,1)S(1)} async-done(((bf16[8,9,2048]{2,1,0:T(8,128)(2,1)}), bf16[8,9,2048]{2,1,0:T(8,128)(2,1)S(1)}, u32[]{:S(2)}, u32[]{:S(2)}) %all-to-all-start.1) | async-done | bytes 294944 | tf_op jit(solution)/shard_map/while/body/eval_jaxpr/all_to_all | solution.py:120
  727.4 14.5 %all-to-all-done = bf16[8,9,2048]{2,1,0:T(8,128)(2,1)S(1)} async-done(((bf16[8,9,2048]{2,1,0:T(8,128)(2,1)}), bf16[8,9,2048]{2,1,0:T(8,128)(2,1)S(1)}, u32[]{:S(2)}, u32[]{:S(2)}) %all-to-all-start) | async-done | bytes 294944 | tf_op jit(solution)/shard_map/while/body/eval_jaxpr/all_to_all | solution.py:121
  741.9 14.1 %conditional.3 = (bf16[72,2048]{1,0:T(8,128)(2,1)S(1)}, bf16[72]{0:T(256)(128)(2,1)S(1)}) conditional(s32[]{:T(128)} %convert_element_type.180, () %tuple.64, (bf16[8,9,2048]{2,1,0:T(8,128)(2,1)S(1)}, bf16[1024,2048]{1,0:T(8,128)(2,1)}, bf16[8,9,2048]{2,1,0:T(8,128)(2,1)S(1)}, bf16[2048,1024]{1,0:T(8,128)(2,1)}, bf16[2048,1024]{1,0:T(8,128)(2,1)}) %tuple.65), branch_computations={%region_6.6_spmd, %region_7.8_spmd} | conditional | flops 1814298624 | bytes 82280696 | solution.py:132
  794.8 13.7 %all-to-all-done.1 = bf16[8,9,2048]{2,1,0:T(8,128)(2,1)S(1)} async-done(((bf16[8,9,2048]{2,1,0:T(8,128)(2,1)}), bf16[8,9,2048]{2,1,0:T(8,128)(2,1)S(1)}, u32[]{:S(2)}, u32[]{:S(2)}) %all-to-all-start.1) | async-done | bytes 294944 | tf_op jit(solution)/shard_map/while/body/eval_jaxpr/all_to_all | solution.py:120
  812.3 14.5 %all-to-all-done = bf16[8,9,2048]{2,1,0:T(8,128)(2,1)S(1)} async-done(((bf16[8,9,2048]{2,1,0:T(8,128)(2,1)}), bf16[8,9,2048]{2,1,0:T(8,128)(2,1)S(1)}, u32[]{:S(2)}, u32[]{:S(2)}) %all-to-all-start) | async-done | bytes 294944 | tf_op jit(solution)/shard_map/while/body/eval_jaxpr/all_to_all | solution.py:121
  841.6 13.0 %all-to-all-done.2 = bf16[8,9,2048]{2,1,0:T(8,128)(2,1)S(1)} async-done(((bf16[8,9,2048]{2,1,0:T(8,128)(2,1)}), bf16[8,9,2048]{2,1,0:T(8,128)(2,1)S(1)}, u32[]{:S(2)}, u32[]{:S(2)}) %all-to-all-start.2) | async-done | bytes 294944 | tf_op jit(solution)/shard_map/while/body/eval_jaxpr/all_to_all | solution.py:134
  868.9 13.7 %all-to-all-done.1 = bf16[8,9,2048]{2,1,0:T(8,128)(2,1)S(1)} async-done(((bf16[8,9,2048]{2,1,0:T(8,128)(2,1)}), bf16[8,9,2048]{2,1,0:T(8,128)(2,1)S(1)}, u32[]{:S(2)}, u32[]{:S(2)}) %all-to-all-start.1) | async-done | bytes 294944 | tf_op jit(solution)/shard_map/while/body/eval_jaxpr/all_to_all | solution.py:120
  886.4 14.5 %all-to-all-done = bf16[8,9,2048]{2,1,0:T(8,128)(2,1)S(1)} async-done(((bf16[8,9,2048]{2,1,0:T(8,128)(2,1)}), bf16[8,9,2048]{2,1,0:T(8,128)(2,1)S(1)}, u32[]{:S(2)}, u32[]{:S(2)}) %all-to-all-start) | async-done | bytes 294944 | tf_op jit(solution)/shard_map/while/body/eval_jaxpr/all_to_all | solution.py:121
  915.6 13.0 %all-to-all-done.2 = bf16[8,9,2048]{2,1,0:T(8,128)(2,1)S(1)} async-done(((bf16[8,9,2048]{2,1,0:T(8,128)(2,1)}), bf16[8,9,2048]{2,1,0:T(8,128)(2,1)S(1)}, u32[]{:S(2)}, u32[]{:S(2)}) %all-to-all-start.2) | async-done | bytes 294944 | tf_op jit(solution)/shard_map/while/body/eval_jaxpr/all_to_all | solution.py:134
  (655 shorter events, 607.4 us)
Async XLA Ops:
  16.6 20.1 %all-to-all-start.1 = ((bf16[8,9,2048]{2,1,0:T(8,128)(2,1)}), bf16[8,9,2048]{2,1,0:T(8,128)(2,1)S(1)}, u32[]{:S(2)}, u32[]{:S(2)}) async-start(bf16[8,9,2048]{2,1,0:T(8,128)(2,1)} %reshape.265), calls=%async_computation.1 | async-start | bytes 1048576 | tf_op jit(solution)/shard_map/while/body/eval_jaxpr/all_to_all | solution.py:120
  36.7 18.2 %all-to-all-start = ((bf16[8,9,2048]{2,1,0:T(8,128)(2,1)}), bf16[8,9,2048]{2,1,0:T(8,128)(2,1)S(1)}, u32[]{:S(2)}, u32[]{:S(2)}) async-start(bf16[8,9,2048]{2,1,0:T(8,128)(2,1)} %reshape.263), calls=%async_computation | async-start | bytes 1048576 | tf_op jit(solution)/shard_map/while/body/eval_jaxpr/all_to_all | solution.py:121
  82.1 13.8 %collective-permute-start = (bf16[16,2048]{1,0:T(8,128)(2,1)S(1)}, bf16[16,2048]{1,0:T(8,128)(2,1)S(1)}, u32[]{:S(2)}, u32[]{:S(2)}) collective-permute-start(bf16[16,2048]{1,0:T(8,128)(2,1)S(1)} %broadcast_select_fusion.2), channel_id=1, source_target_pairs={{8,0},{16,8},{24,16},{9,1},{17,9},{25,17},{10,2},{18,10},{26,18},{... | collective-permute-start | bytes 196616 | tf_op jit(solution)/shard_map/while/body/eval_jaxpr/ppermute | solution.py:10
  91.1 14.7 %all-to-all-start.1 = ((bf16[8,9,2048]{2,1,0:T(8,128)(2,1)}), bf16[8,9,2048]{2,1,0:T(8,128)(2,1)S(1)}, u32[]{:S(2)}, u32[]{:S(2)}) async-start(bf16[8,9,2048]{2,1,0:T(8,128)(2,1)} %reshape.265), calls=%async_computation.1 | async-start | bytes 1048576 | tf_op jit(solution)/shard_map/while/body/eval_jaxpr/all_to_all | solution.py:120
  105.8 14.3 %all-to-all-start = ((bf16[8,9,2048]{2,1,0:T(8,128)(2,1)}), bf16[8,9,2048]{2,1,0:T(8,128)(2,1)S(1)}, u32[]{:S(2)}, u32[]{:S(2)}) async-start(bf16[8,9,2048]{2,1,0:T(8,128)(2,1)} %reshape.263), calls=%async_computation | async-start | bytes 1048576 | tf_op jit(solution)/shard_map/while/body/eval_jaxpr/all_to_all | solution.py:121
  147.4 18.9 %all-to-all-start.2 = ((bf16[8,9,2048]{2,1,0:T(8,128)(2,1)}), bf16[8,9,2048]{2,1,0:T(8,128)(2,1)S(1)}, u32[]{:S(2)}, u32[]{:S(2)}) async-start(bf16[8,9,2048]{2,1,0:T(8,128)(2,1)} %reshape.266), calls=%async_computation.2 | async-start | bytes 1048576 | tf_op jit(solution)/shard_map/while/body/eval_jaxpr/all_to_all | solution.py:134
  175.3 19.2 %all-to-all-start.1 = ((bf16[8,9,2048]{2,1,0:T(8,128)(2,1)}), bf16[8,9,2048]{2,1,0:T(8,128)(2,1)S(1)}, u32[]{:S(2)}, u32[]{:S(2)}) async-start(bf16[8,9,2048]{2,1,0:T(8,128)(2,1)} %reshape.265), calls=%async_computation.1 | async-start | bytes 1048576 | tf_op jit(solution)/shard_map/while/body/eval_jaxpr/all_to_all | solution.py:120
  194.6 18.3 %all-to-all-start = ((bf16[8,9,2048]{2,1,0:T(8,128)(2,1)}), bf16[8,9,2048]{2,1,0:T(8,128)(2,1)S(1)}, u32[]{:S(2)}, u32[]{:S(2)}) async-start(bf16[8,9,2048]{2,1,0:T(8,128)(2,1)} %reshape.263), calls=%async_computation | async-start | bytes 1048576 | tf_op jit(solution)/shard_map/while/body/eval_jaxpr/all_to_all | solution.py:121
  237.9 16.9 %all-to-all-start.2 = ((bf16[8,9,2048]{2,1,0:T(8,128)(2,1)}), bf16[8,9,2048]{2,1,0:T(8,128)(2,1)S(1)}, u32[]{:S(2)}, u32[]{:S(2)}) async-start(bf16[8,9,2048]{2,1,0:T(8,128)(2,1)} %reshape.266), calls=%async_computation.2 | async-start | bytes 1048576 | tf_op jit(solution)/shard_map/while/body/eval_jaxpr/all_to_all | solution.py:134
  263.9 18.8 %all-to-all-start.1 = ((bf16[8,9,2048]{2,1,0:T(8,128)(2,1)}), bf16[8,9,2048]{2,1,0:T(8,128)(2,1)S(1)}, u32[]{:S(2)}, u32[]{:S(2)}) async-start(bf16[8,9,2048]{2,1,0:T(8,128)(2,1)} %reshape.265), calls=%async_computation.1 | async-start | bytes 1048576 | tf_op jit(solution)/shard_map/while/body/eval_jaxpr/all_to_all | solution.py:120
  282.8 18.3 %all-to-all-start = ((bf16[8,9,2048]{2,1,0:T(8,128)(2,1)}), bf16[8,9,2048]{2,1,0:T(8,128)(2,1)S(1)}, u32[]{:S(2)}, u32[]{:S(2)}) async-start(bf16[8,9,2048]{2,1,0:T(8,128)(2,1)} %reshape.263), calls=%async_computation | async-start | bytes 1048576 | tf_op jit(solution)/shard_map/while/body/eval_jaxpr/all_to_all | solution.py:121
  326.0 16.9 %all-to-all-start.2 = ((bf16[8,9,2048]{2,1,0:T(8,128)(2,1)}), bf16[8,9,2048]{2,1,0:T(8,128)(2,1)S(1)}, u32[]{:S(2)}, u32[]{:S(2)}) async-start(bf16[8,9,2048]{2,1,0:T(8,128)(2,1)} %reshape.266), calls=%async_computation.2 | async-start | bytes 1048576 | tf_op jit(solution)/shard_map/while/body/eval_jaxpr/all_to_all | solution.py:134
  352.1 18.8 %all-to-all-start.1 = ((bf16[8,9,2048]{2,1,0:T(8,128)(2,1)}), bf16[8,9,2048]{2,1,0:T(8,128)(2,1)S(1)}, u32[]{:S(2)}, u32[]{:S(2)}) async-start(bf16[8,9,2048]{2,1,0:T(8,128)(2,1)} %reshape.265), calls=%async_computation.1 | async-start | bytes 1048576 | tf_op jit(solution)/shard_map/while/body/eval_jaxpr/all_to_all | solution.py:120
  370.9 18.3 %all-to-all-start = ((bf16[8,9,2048]{2,1,0:T(8,128)(2,1)}), bf16[8,9,2048]{2,1,0:T(8,128)(2,1)S(1)}, u32[]{:S(2)}, u32[]{:S(2)}) async-start(bf16[8,9,2048]{2,1,0:T(8,128)(2,1)} %reshape.263), calls=%async_computation | async-start | bytes 1048576 | tf_op jit(solution)/shard_map/while/body/eval_jaxpr/all_to_all | solution.py:121
  414.2 16.9 %all-to-all-start.2 = ((bf16[8,9,2048]{2,1,0:T(8,128)(2,1)}), bf16[8,9,2048]{2,1,0:T(8,128)(2,1)S(1)}, u32[]{:S(2)}, u32[]{:S(2)}) async-start(bf16[8,9,2048]{2,1,0:T(8,128)(2,1)} %reshape.266), calls=%async_computation.2 | async-start | bytes 1048576 | tf_op jit(solution)/shard_map/while/body/eval_jaxpr/all_to_all | solution.py:134
  440.2 18.8 %all-to-all-start.1 = ((bf16[8,9,2048]{2,1,0:T(8,128)(2,1)}), bf16[8,9,2048]{2,1,0:T(8,128)(2,1)S(1)}, u32[]{:S(2)}, u32[]{:S(2)}) async-start(bf16[8,9,2048]{2,1,0:T(8,128)(2,1)} %reshape.265), calls=%async_computation.1 | async-start | bytes 1048576 | tf_op jit(solution)/shard_map/while/body/eval_jaxpr/all_to_all | solution.py:120
  459.1 18.3 %all-to-all-start = ((bf16[8,9,2048]{2,1,0:T(8,128)(2,1)}), bf16[8,9,2048]{2,1,0:T(8,128)(2,1)S(1)}, u32[]{:S(2)}, u32[]{:S(2)}) async-start(bf16[8,9,2048]{2,1,0:T(8,128)(2,1)} %reshape.263), calls=%async_computation | async-start | bytes 1048576 | tf_op jit(solution)/shard_map/while/body/eval_jaxpr/all_to_all | solution.py:121
  502.3 16.9 %all-to-all-start.2 = ((bf16[8,9,2048]{2,1,0:T(8,128)(2,1)}), bf16[8,9,2048]{2,1,0:T(8,128)(2,1)S(1)}, u32[]{:S(2)}, u32[]{:S(2)}) async-start(bf16[8,9,2048]{2,1,0:T(8,128)(2,1)} %reshape.266), calls=%async_computation.2 | async-start | bytes 1048576 | tf_op jit(solution)/shard_map/while/body/eval_jaxpr/all_to_all | solution.py:134
  528.4 18.8 %all-to-all-start.1 = ((bf16[8,9,2048]{2,1,0:T(8,128)(2,1)}), bf16[8,9,2048]{2,1,0:T(8,128)(2,1)S(1)}, u32[]{:S(2)}, u32[]{:S(2)}) async-start(bf16[8,9,2048]{2,1,0:T(8,128)(2,1)} %reshape.265), calls=%async_computation.1 | async-start | bytes 1048576 | tf_op jit(solution)/shard_map/while/body/eval_jaxpr/all_to_all | solution.py:120
  547.2 18.3 %all-to-all-start = ((bf16[8,9,2048]{2,1,0:T(8,128)(2,1)}), bf16[8,9,2048]{2,1,0:T(8,128)(2,1)S(1)}, u32[]{:S(2)}, u32[]{:S(2)}) async-start(bf16[8,9,2048]{2,1,0:T(8,128)(2,1)} %reshape.263), calls=%async_computation | async-start | bytes 1048576 | tf_op jit(solution)/shard_map/while/body/eval_jaxpr/all_to_all | solution.py:121
  590.5 16.9 %all-to-all-start.2 = ((bf16[8,9,2048]{2,1,0:T(8,128)(2,1)}), bf16[8,9,2048]{2,1,0:T(8,128)(2,1)S(1)}, u32[]{:S(2)}, u32[]{:S(2)}) async-start(bf16[8,9,2048]{2,1,0:T(8,128)(2,1)} %reshape.266), calls=%async_computation.2 | async-start | bytes 1048576 | tf_op jit(solution)/shard_map/while/body/eval_jaxpr/all_to_all | solution.py:134
  616.5 18.8 %all-to-all-start.1 = ((bf16[8,9,2048]{2,1,0:T(8,128)(2,1)}), bf16[8,9,2048]{2,1,0:T(8,128)(2,1)S(1)}, u32[]{:S(2)}, u32[]{:S(2)}) async-start(bf16[8,9,2048]{2,1,0:T(8,128)(2,1)} %reshape.265), calls=%async_computation.1 | async-start | bytes 1048576 | tf_op jit(solution)/shard_map/while/body/eval_jaxpr/all_to_all | solution.py:120
  635.4 18.3 %all-to-all-start = ((bf16[8,9,2048]{2,1,0:T(8,128)(2,1)}), bf16[8,9,2048]{2,1,0:T(8,128)(2,1)S(1)}, u32[]{:S(2)}, u32[]{:S(2)}) async-start(bf16[8,9,2048]{2,1,0:T(8,128)(2,1)} %reshape.263), calls=%async_computation | async-start | bytes 1048576 | tf_op jit(solution)/shard_map/while/body/eval_jaxpr/all_to_all | solution.py:121
  678.7 16.9 %all-to-all-start.2 = ((bf16[8,9,2048]{2,1,0:T(8,128)(2,1)}), bf16[8,9,2048]{2,1,0:T(8,128)(2,1)S(1)}, u32[]{:S(2)}, u32[]{:S(2)}) async-start(bf16[8,9,2048]{2,1,0:T(8,128)(2,1)} %reshape.266), calls=%async_computation.2 | async-start | bytes 1048576 | tf_op jit(solution)/shard_map/while/body/eval_jaxpr/all_to_all | solution.py:134
  704.7 18.8 %all-to-all-start.1 = ((bf16[8,9,2048]{2,1,0:T(8,128)(2,1)}), bf16[8,9,2048]{2,1,0:T(8,128)(2,1)S(1)}, u32[]{:S(2)}, u32[]{:S(2)}) async-start(bf16[8,9,2048]{2,1,0:T(8,128)(2,1)} %reshape.265), calls=%async_computation.1 | async-start | bytes 1048576 | tf_op jit(solution)/shard_map/while/body/eval_jaxpr/all_to_all | solution.py:120
  723.6 18.3 %all-to-all-start = ((bf16[8,9,2048]{2,1,0:T(8,128)(2,1)}), bf16[8,9,2048]{2,1,0:T(8,128)(2,1)S(1)}, u32[]{:S(2)}, u32[]{:S(2)}) async-start(bf16[8,9,2048]{2,1,0:T(8,128)(2,1)} %reshape.263), calls=%async_computation | async-start | bytes 1048576 | tf_op jit(solution)/shard_map/while/body/eval_jaxpr/all_to_all | solution.py:121
  789.6 18.8 %all-to-all-start.1 = ((bf16[8,9,2048]{2,1,0:T(8,128)(2,1)}), bf16[8,9,2048]{2,1,0:T(8,128)(2,1)S(1)}, u32[]{:S(2)}, u32[]{:S(2)}) async-start(bf16[8,9,2048]{2,1,0:T(8,128)(2,1)} %reshape.265), calls=%async_computation.1 | async-start | bytes 1048576 | tf_op jit(solution)/shard_map/while/body/eval_jaxpr/all_to_all | solution.py:120
  808.5 18.3 %all-to-all-start = ((bf16[8,9,2048]{2,1,0:T(8,128)(2,1)}), bf16[8,9,2048]{2,1,0:T(8,128)(2,1)S(1)}, u32[]{:S(2)}, u32[]{:S(2)}) async-start(bf16[8,9,2048]{2,1,0:T(8,128)(2,1)} %reshape.263), calls=%async_computation | async-start | bytes 1048576 | tf_op jit(solution)/shard_map/while/body/eval_jaxpr/all_to_all | solution.py:121
  837.7 16.9 %all-to-all-start.2 = ((bf16[8,9,2048]{2,1,0:T(8,128)(2,1)}), bf16[8,9,2048]{2,1,0:T(8,128)(2,1)S(1)}, u32[]{:S(2)}, u32[]{:S(2)}) async-start(bf16[8,9,2048]{2,1,0:T(8,128)(2,1)} %reshape.266), calls=%async_computation.2 | async-start | bytes 1048576 | tf_op jit(solution)/shard_map/while/body/eval_jaxpr/all_to_all | solution.py:134
  863.7 18.8 %all-to-all-start.1 = ((bf16[8,9,2048]{2,1,0:T(8,128)(2,1)}), bf16[8,9,2048]{2,1,0:T(8,128)(2,1)S(1)}, u32[]{:S(2)}, u32[]{:S(2)}) async-start(bf16[8,9,2048]{2,1,0:T(8,128)(2,1)} %reshape.265), calls=%async_computation.1 | async-start | bytes 1048576 | tf_op jit(solution)/shard_map/while/body/eval_jaxpr/all_to_all | solution.py:120
  882.6 18.3 %all-to-all-start = ((bf16[8,9,2048]{2,1,0:T(8,128)(2,1)}), bf16[8,9,2048]{2,1,0:T(8,128)(2,1)S(1)}, u32[]{:S(2)}, u32[]{:S(2)}) async-start(bf16[8,9,2048]{2,1,0:T(8,128)(2,1)} %reshape.263), calls=%async_computation | async-start | bytes 1048576 | tf_op jit(solution)/shard_map/while/body/eval_jaxpr/all_to_all | solution.py:121
  911.7 16.9 %all-to-all-start.2 = ((bf16[8,9,2048]{2,1,0:T(8,128)(2,1)}), bf16[8,9,2048]{2,1,0:T(8,128)(2,1)S(1)}, u32[]{:S(2)}, u32[]{:S(2)}) async-start(bf16[8,9,2048]{2,1,0:T(8,128)(2,1)} %reshape.266), calls=%async_computation.2 | async-start | bytes 1048576 | tf_op jit(solution)/shard_map/while/body/eval_jaxpr/all_to_all | solution.py:134
  (59 other events, 670.3 us)
where the time goes:
time: 939 us; the launch traced here: 932 us
  waiting for transfers between devices  498 us (53%)
  starting transfers between devices  189 us (20%)
  matrix products  138 us (15%)
  local copies, waits for them, and re-layouts  60.3 us (6%)
  other arithmetic  37.8 us (4%)
    all_to_all x11, waiting for transfers between devices, advance(): lax.all_to_all(sent_grad, 'expert', split_axis=0, concat_axis=0, tiled=True)  155 us
    all_to_all x11, waiting for transfers between devices, advance(): lax.all_to_all(sent_normed, 'expert', split_axis=0, concat_axis=0, tiled=...  144 us
    all_to_all x11, waiting for transfers between devices, advance(): lax.all_to_all(returned.reshape(experts, capacity, width), 'expert', spli...  139 us
    all_to_all x11, waiting for transfers between devices, advance(): lax.all_to_all(dprob.reshape(experts, capacity).astype(jnp.bfloat16), 'ex...  58.5 us
    all_to_all x11, starting transfers between devices, advance(): lax.all_to_all(sent_normed, 'expert', split_axis=0, concat_axis=0, tiled=...  43.6 us
    all_to_all x11, starting transfers between devices, advance(): lax.all_to_all(dprob.reshape(experts, capacity).astype(jnp.bfloat16), 'ex...  42.3 us
    all_to_all x11, starting transfers between devices, advance(): lax.all_to_all(sent_grad, 'expert', split_axis=0, concat_axis=0, tiled=True)  39.9 us
    all_to_all x11, starting transfers between devices, advance(): lax.all_to_all(returned.reshape(experts, capacity, width), 'expert', spli...  38.4 us
  transfers between devices with their start and end apart: 55, of which 45 were waited for; matrix products, arithmetic and copies ran while one was open for 9% of the time, Pallas kernels for 0%

commit v1 on v0

v1 whole, which is shorter than its diff:
```python
import jax
import jax.numpy as jnp
from jax import lax
from jax.sharding import PartitionSpec as P

CHUNK = 2


def shifted(shard, axis, by):
    devices = lax.axis_size(axis)
    pairs = [(i, i + by) for i in range(devices) if 0 <= i + by < devices]
    return lax.ppermute(shard, axis, pairs)


def prepare(x_rows, gain):
    x_float = x_rows.astype(jnp.float32)
    inverse = lax.rsqrt(jnp.mean(x_float * x_float, axis=-1, keepdims=True) + 1e-05)
    normed = (x_float * inverse * gain).astype(jnp.bfloat16)
    return (x_float, inverse, normed)


def selection(ids, experts, capacity):
    pair_ids = ids.reshape(-1)
    onehot = (pair_ids[:, None] == jnp.arange(experts, dtype=jnp.int32)[None, :]).astype(jnp.int32)
    ranks = jnp.sum(onehot * (jnp.cumsum(onehot, axis=0) - 1), axis=1)
    target = pair_ids * capacity + ranks
    return (target[:, None] == jnp.arange(experts * capacity, dtype=jnp.int32)[None, :]).astype(
        jnp.bfloat16
    )


def pack_rows(select, rows, per_token):
    repeated = jnp.repeat(rows, per_token, axis=1)
    packed = jnp.einsum("mps,mpw->msw", select, repeated, preferred_element_type=jnp.float32)
    return packed.astype(jnp.bfloat16)


def finish(x_float, inverse, gain, router_layer, probs, choose, picked, grad_in, pair_back, pair_prob):
    dfull = jnp.sum(pair_prob[..., None] * choose, axis=-2)
    dlogit = probs * (dfull - jnp.sum(probs * dfull, axis=-1, keepdims=True))
    router_term = jnp.dot(
        dlogit, router_layer.astype(jnp.float32).T, precision=lax.Precision.HIGHEST
    )
    dnormed = jnp.sum(picked[..., None] * pair_back, axis=-2) + router_term
    scaled = gain * dnormed
    inner = jnp.mean(x_float * scaled, axis=-1, keepdims=True)
    result = (
        grad_in.astype(jnp.float32)
        + inverse * scaled
        - x_float * inverse * inverse * inverse * inner
    )
    return result.astype(jnp.bfloat16)


def shards(layer_inputs, top_grad, expert_ids, router, norm_gain, w_gate, w_up, w_down):
    segments = lax.axis_size("section")
    experts = lax.axis_size("expert")
    segment_index = lax.axis_index("section")
    micro = layer_inputs.shape[1]
    tok_rows = layer_inputs.shape[2]
    width = layer_inputs.shape[3]
    per_token = expert_ids.shape[3]
    capacity = min(tok_rows, per_token * tok_rows // experts + max(1, tok_rows // 16))
    slots = experts * capacity
    chunk = CHUNK if micro % CHUNK == 0 else 1
    chunks = micro // chunk
    lanes = 128
    gain = norm_gain[0].astype(jnp.float32)
    router_layer = router[0]
    gate_w = w_gate[0, 0]
    up_w = w_up[0, 0]
    down_w = w_down[0, 0]
    ids = expert_ids[0]
    x_float, inverse, normed = prepare(layer_inputs[0], gain)
    top_full = lax.all_gather(top_grad, "section", axis=0, tiled=True)

    select = jax.vmap(lambda i: selection(i, experts, capacity))(ids)
    sent_normed = pack_rows(select, normed, per_token).reshape(micro, experts, capacity, width)
    got_normed = lax.all_to_all(sent_normed, "expert", split_axis=1, concat_axis=1, tiled=True)
    rows = got_normed.reshape(micro * slots, width)
    gate = jnp.dot(rows, gate_w, preferred_element_type=jnp.float32)
    up_rows = jnp.dot(rows, up_w, preferred_element_type=jnp.float32)
    squash = jax.nn.sigmoid(gate)
    active = gate * squash
    hidden = (active * up_rows).astype(jnp.bfloat16)
    output = jnp.dot(hidden, down_w, preferred_element_type=jnp.float32)
    factor = up_rows * squash * (1.0 + gate * (1.0 - squash))
    output = output.reshape(micro, slots, width)
    factor = factor.reshape(micro, slots, -1)
    active = active.reshape(micro, slots, -1)

    logits = jnp.dot(normed, router_layer, preferred_element_type=jnp.float32)
    raised = jnp.exp(logits)
    probs = raised / jnp.sum(raised, axis=-1, keepdims=True)
    choose = (ids[..., None] == jnp.arange(router_layer.shape[1], dtype=jnp.int32)).astype(
        jnp.float32
    )
    picked = jnp.sum(probs[..., None, :] * choose, axis=-1)

    def take(values, start):
        return lax.dynamic_slice_in_dim(values, start, chunk, 0)

    def advance(step, carry):
        previous, collected = carry
        arrived = shifted(previous, "section", -1)
        position = step - (segments - 1 - segment_index)
        working = jnp.logical_and(position >= 0, position < chunks)
        start = jnp.clip(position, 0, chunks - 1) * chunk
        grad_in = jnp.where(segment_index == segments - 1, take(top_full, start), arrived)
        select_now = take(select, start)
        sent_grad = pack_rows(select_now, grad_in, per_token).reshape(
            chunk, experts, capacity, width
        )
        got_grad = lax.all_to_all(sent_grad, "expert", split_axis=1, concat_axis=1, tiled=True)
        rows_grad = got_grad.reshape(chunk * slots, width)
        out_now = take(output, start).reshape(chunk * slots, width)
        dprob = jnp.sum(out_now * rows_grad.astype(jnp.float32), axis=-1)
        dhidden = lax.dot_general(
            rows_grad, down_w, (((1,), (1,)), ((), ())), preferred_element_type=jnp.float32
        )
        factor_now = take(factor, start).reshape(chunk * slots, -1)
        active_now = take(active, start).reshape(chunk * slots, -1)
        dgate = (dhidden * factor_now).astype(jnp.bfloat16)
        dup = (dhidden * active_now).astype(jnp.bfloat16)
        returned = lax.dot_general(
            dgate, gate_w, (((1,), (1,)), ((), ())), preferred_element_type=jnp.float32
        )
        returned = returned + lax.dot_general(
            dup, up_w, (((1,), (1,)), ((), ())), preferred_element_type=jnp.float32
        )
        high = dprob.astype(jnp.bfloat16)
        low = (dprob - high.astype(jnp.float32)).astype(jnp.bfloat16)
        column = lax.broadcasted_iota(jnp.int32, (chunk * slots, lanes), 1)
        extra = jnp.where(column == 0, high[:, None], jnp.where(column == 1, low[:, None], 0))
        packed = jnp.concatenate([returned.astype(jnp.bfloat16), extra.astype(jnp.bfloat16)], axis=1)
        packed = packed.reshape(chunk, experts, capacity, width + lanes)
        back = lax.all_to_all(packed, "expert", split_axis=1, concat_axis=1, tiled=True)
        back = back.reshape(chunk, slots, width + lanes)
        pair = jnp.einsum("mps,msw->mpw", select_now, back, preferred_element_type=jnp.float32)
        pair_back = pair[..., :width].reshape(chunk, tok_rows, per_token, width)
        pair_prob = (pair[..., width] + pair[..., width + 1]).reshape(chunk, tok_rows, per_token)
        result = finish(
            take(x_float, start),
            take(inverse, start),
            gain,
            router_layer,
            take(probs, start),
            take(choose, start),
            take(picked, start),
            grad_in,
            pair_back,
            pair_prob,
        )
        retained = take(collected, start)
        collected = lax.dynamic_update_slice_in_dim(
            collected, jnp.where(working, result, retained), start, 0
        )
        return (result, collected)

    begin = (
        jnp.zeros((chunk, tok_rows, width), jnp.bfloat16),
        jnp.zeros((micro, tok_rows, width), jnp.bfloat16),
    )
    final_grad, collected = lax.fori_loop(0, chunks + segments - 1, advance, begin)
    return collected.reshape(1, micro, tok_rows, width)


def solution(mesh):
    placed = (
        P("section", None, "expert", None),
        P("section", "expert", None),
        P("section", None, "expert", None),
        P("section", None, None),
        P("section", None),
        P("section", "expert", None, None),
        P("section", "expert", None, None),
        P("section", "expert", None, None),
    )
    return jax.shard_map(
        shards,
        mesh=mesh,
        in_specs=placed,
        out_specs=P("section", None, "expert", None),
        check_vma=False,
    )
```

time: 939 us -> 570 us (0.61)
  the two profiles are of different devices: /device:TPU:2 before, /device:TPU:0 now
where the time goes in v1:
time: 570 us; the launch traced here: 566 us
  waiting for transfers between devices  269 us (47%)
  matrix products  80.2 us (14%)
  starting transfers between devices  78 us (14%)
  local copies, waits for them, and re-layouts  67.5 us (12%)
  other arithmetic  62.1 us (11%)
  blocking collectives  7.61 us (1%)
    all_to_all x7, waiting for transfers between devices, advance(): lax.all_to_all(packed, 'expert', split_axis=1, concat_axis=1, tiled=True)  114 us
    all_to_all x7, waiting for transfers between devices, advance(): lax.all_to_all(sent_grad, 'expert', split_axis=1, concat_axis=1, tiled=True)  99.5 us
    all_to_all x1, waiting for transfers between devices, shards(): lax.all_to_all(sent_normed, 'expert', split_axis=1, concat_axis=1, tiled=...  42.1 us
    all_to_all x7, starting transfers between devices, advance(): lax.all_to_all(packed, 'expert', split_axis=1, concat_axis=1, tiled=True)  36.2 us
    dot_general x7, matrix products, advance(): lax.dot_general(rows_grad, down_w, (((1,), (1,)), ((), ())), preferred_el...  27 us
    all_to_all x7, starting transfers between devices, advance(): lax.all_to_all(sent_grad, 'expert', split_axis=1, concat_axis=1, tiled=True)  25.3 us
    reduce_sum x7, other arithmetic, advance(): dprob = jnp.sum(out_now * rows_grad.astype(jnp.float32), axis=-1)  23.3 us
    dynamic_slice x21, local copies, waits for them, and re-layouts, take(): return lax.dynamic_slice_in_dim(values, start, chunk, 0)  14.7 us
  transfers between devices with their start and end apart: 22, of which 22 were waited for; matrix products, arithmetic and copies ran while one was open for 3% of the time, Pallas kernels for 0%

profile of v1, /device:TPU:0, one launch (start us, length us, event | category | flops | bytes accessed | tf_op | source)
XLA Modules:
  0.0 565.8 jit_solution(13926109914055575953)
XLA Ops:
  13.7 7.4 %all-to-all-start.2 = ((bf16[8,8,9,2048]{3,0,2,1:T(8,128)(2,1)}), bf16[8,8,9,2048]{3,0,2,1:T(8,128)(2,1)S(1)}, u32[]{:S(2)}, u32[]{:S(2)}) async-start(bf16[8,8,9,2048]{3,0,2,1:T(8,128)(2,1)} %bitcast.100), calls=%async_computation.2 | async-start | bytes 4718592 | tf_op jit(solution)/shard_map/all_to_all | solution.py:79
  23.4 7.6 %all_gather.3 = bf16[8,16,2048]{2,1,0:T(8,128)(2,1)} all-gather(bf16[2,16,2048]{2,1,0:T(8,128)(2,1)S(1)} %copy-done.9), channel_id=1, replica_groups=mesh['section'=4,'expert'=8] {'section'}, dimensions={0}, use_global_device_ids=true | all-gather | bytes 655360 | tf_op jit(solution)/shard_map/all_gather | solution.py:75
  32.9 42.1 %all-to-all-done.2 = bf16[8,8,9,2048]{3,0,2,1:T(8,128)(2,1)S(1)} async-done(((bf16[8,8,9,2048]{3,0,2,1:T(8,128)(2,1)}), bf16[8,8,9,2048]{3,0,2,1:T(8,128)(2,1)S(1)}, u32[]{:S(2)}, u32[]{:S(2)}) %all-to-all-start.2) | async-done | bytes 2359328 | tf_op jit(solution)/shard_map/all_to_all | solution.py:79
  81.8 4.5 fusion.38
  86.4 5.0 multiply_convert_fusion
  91.4 5.3 fusion.19
  97.5 468.4 %while.18 = (s32[]{:T(128)}, bf16[2,16,2048]{2,1,0:T(8,128)(2,1)S(1)}, bf16[8,16,2048]{2,1,0:T(8,128)(2,1)}, pred[]{:T(512)}, s32[]{:T(128)}, /*index=5*/bf16[8,...) while((s32[]{:T(128)}, ...), condition=%wide.region_11.12_spmd.clone, body=%wide.region_5.11_spmd.clone.sunk | while | flops 1901248128 | bytes 84584528 | solution.py:164
  108.8 14.2 %all-to-all-done = bf16[2,8,9,2048]{3,0,2,1:T(2,128)(2,1)S(1)} async-done(((bf16[2,8,9,2048]{3,0,2,1:T(2,128)(2,1)}), bf16[2,8,9,2048]{3,0,2,1:T(2,128)(2,1)S(1)}, u32[]{:S(2)}, u32[]{:S(2)}) %all-to-all-start) | async-done | bytes 589856 | tf_op jit(solution)/shard_map/while/body/eval_jaxpr/all_to_all | solution.py:114
  127.1 3.9 fusion.87
  136.6 5.2 all-to-all-start.1
  142.6 16.3 %all-to-all-done.1 = bf16[2,8,9,2176]{3,0,2,1:T(2,128)(2,1)S(1)} async-done(((bf16[2,8,9,2176]{3,0,2,1:T(2,128)(2,1)}), bf16[2,8,9,2176]{3,0,2,1:T(2,128)(2,1)S(1)}, u32[]{:S(2)}, u32[]{:S(2)}) %all-to-all-start.1) | async-done | bytes 626720 | tf_op jit(solution)/shard_map/while/body/eval_jaxpr/all_to_all | solution.py:137
  175.7 14.2 %all-to-all-done = bf16[2,8,9,2048]{3,0,2,1:T(2,128)(2,1)S(1)} async-done(((bf16[2,8,9,2048]{3,0,2,1:T(2,128)(2,1)}), bf16[2,8,9,2048]{3,0,2,1:T(2,128)(2,1)S(1)}, u32[]{:S(2)}, u32[]{:S(2)}) %all-to-all-start) | async-done | bytes 589856 | tf_op jit(solution)/shard_map/while/body/eval_jaxpr/all_to_all | solution.py:114
  194.0 3.9 fusion.87
  203.5 5.2 all-to-all-start.1
  209.5 16.3 %all-to-all-done.1 = bf16[2,8,9,2176]{3,0,2,1:T(2,128)(2,1)S(1)} async-done(((bf16[2,8,9,2176]{3,0,2,1:T(2,128)(2,1)}), bf16[2,8,9,2176]{3,0,2,1:T(2,128)(2,1)S(1)}, u32[]{:S(2)}, u32[]{:S(2)}) %all-to-all-start.1) | async-done | bytes 626720 | tf_op jit(solution)/shard_map/while/body/eval_jaxpr/all_to_all | solution.py:137
  242.6 14.2 %all-to-all-done = bf16[2,8,9,2048]{3,0,2,1:T(2,128)(2,1)S(1)} async-done(((bf16[2,8,9,2048]{3,0,2,1:T(2,128)(2,1)}), bf16[2,8,9,2048]{3,0,2,1:T(2,128)(2,1)S(1)}, u32[]{:S(2)}, u32[]{:S(2)}) %all-to-all-start) | async-done | bytes 589856 | tf_op jit(solution)/shard_map/while/body/eval_jaxpr/all_to_all | solution.py:114
  260.9 3.9 fusion.87
  270.5 5.2 all-to-all-start.1
  276.4 16.3 %all-to-all-done.1 = bf16[2,8,9,2176]{3,0,2,1:T(2,128)(2,1)S(1)} async-done(((bf16[2,8,9,2176]{3,0,2,1:T(2,128)(2,1)}), bf16[2,8,9,2176]{3,0,2,1:T(2,128)(2,1)S(1)}, u32[]{:S(2)}, u32[]{:S(2)}) %all-to-all-start.1) | async-done | bytes 626720 | tf_op jit(solution)/shard_map/while/body/eval_jaxpr/all_to_all | solution.py:137
  309.5 14.2 %all-to-all-done = bf16[2,8,9,2048]{3,0,2,1:T(2,128)(2,1)S(1)} async-done(((bf16[2,8,9,2048]{3,0,2,1:T(2,128)(2,1)}), bf16[2,8,9,2048]{3,0,2,1:T(2,128)(2,1)S(1)}, u32[]{:S(2)}, u32[]{:S(2)}) %all-to-all-start) | async-done | bytes 589856 | tf_op jit(solution)/shard_map/while/body/eval_jaxpr/all_to_all | solution.py:114
  327.8 3.9 fusion.87
  337.4 5.2 all-to-all-start.1
  343.3 16.3 %all-to-all-done.1 = bf16[2,8,9,2176]{3,0,2,1:T(2,128)(2,1)S(1)} async-done(((bf16[2,8,9,2176]{3,0,2,1:T(2,128)(2,1)}), bf16[2,8,9,2176]{3,0,2,1:T(2,128)(2,1)S(1)}, u32[]{:S(2)}, u32[]{:S(2)}) %all-to-all-start.1) | async-done | bytes 626720 | tf_op jit(solution)/shard_map/while/body/eval_jaxpr/all_to_all | solution.py:137
  376.4 14.2 %all-to-all-done = bf16[2,8,9,2048]{3,0,2,1:T(2,128)(2,1)S(1)} async-done(((bf16[2,8,9,2048]{3,0,2,1:T(2,128)(2,1)}), bf16[2,8,9,2048]{3,0,2,1:T(2,128)(2,1)S(1)}, u32[]{:S(2)}, u32[]{:S(2)}) %all-to-all-start) | async-done | bytes 589856 | tf_op jit(solution)/shard_map/while/body/eval_jaxpr/all_to_all | solution.py:114
  404.3 5.2 all-to-all-start.1
  410.2 16.3 %all-to-all-done.1 = bf16[2,8,9,2176]{3,0,2,1:T(2,128)(2,1)S(1)} async-done(((bf16[2,8,9,2176]{3,0,2,1:T(2,128)(2,1)}), bf16[2,8,9,2176]{3,0,2,1:T(2,128)(2,1)S(1)}, u32[]{:S(2)}, u32[]{:S(2)}) %all-to-all-start.1) | async-done | bytes 626720 | tf_op jit(solution)/shard_map/while/body/eval_jaxpr/all_to_all | solution.py:137
  443.3 14.2 %all-to-all-done = bf16[2,8,9,2048]{3,0,2,1:T(2,128)(2,1)S(1)} async-done(((bf16[2,8,9,2048]{3,0,2,1:T(2,128)(2,1)}), bf16[2,8,9,2048]{3,0,2,1:T(2,128)(2,1)S(1)}, u32[]{:S(2)}, u32[]{:S(2)}) %all-to-all-start) | async-done | bytes 589856 | tf_op jit(solution)/shard_map/while/body/eval_jaxpr/all_to_all | solution.py:114
  471.2 5.2 all-to-all-start.1
  477.1 16.3 %all-to-all-done.1 = bf16[2,8,9,2176]{3,0,2,1:T(2,128)(2,1)S(1)} async-done(((bf16[2,8,9,2176]{3,0,2,1:T(2,128)(2,1)}), bf16[2,8,9,2176]{3,0,2,1:T(2,128)(2,1)S(1)}, u32[]{:S(2)}, u32[]{:S(2)}) %all-to-all-start.1) | async-done | bytes 626720 | tf_op jit(solution)/shard_map/while/body/eval_jaxpr/all_to_all | solution.py:137
  510.2 14.2 %all-to-all-done = bf16[2,8,9,2048]{3,0,2,1:T(2,128)(2,1)S(1)} async-done(((bf16[2,8,9,2048]{3,0,2,1:T(2,128)(2,1)}), bf16[2,8,9,2048]{3,0,2,1:T(2,128)(2,1)S(1)}, u32[]{:S(2)}, u32[]{:S(2)}) %all-to-all-start) | async-done | bytes 589856 | tf_op jit(solution)/shard_map/while/body/eval_jaxpr/all_to_all | solution.py:114
  538.1 5.2 all-to-all-start.1
  544.0 16.3 %all-to-all-done.1 = bf16[2,8,9,2176]{3,0,2,1:T(2,128)(2,1)S(1)} async-done(((bf16[2,8,9,2176]{3,0,2,1:T(2,128)(2,1)}), bf16[2,8,9,2176]{3,0,2,1:T(2,128)(2,1)S(1)}, u32[]{:S(2)}, u32[]{:S(2)}) %all-to-all-start.1) | async-done | bytes 626720 | tf_op jit(solution)/shard_map/while/body/eval_jaxpr/all_to_all | solution.py:137
  (358 shorter events, 227.5 us)
Async XLA Ops:
  13.7 7.5 %copy-start.5 = (bf16[1,8,16,2048]{3,2,1,0:T(8,128)(2,1)S(1)}, bf16[1,8,16,2048]{3,2,1,0:T(8,128)(2,1)}, u32[]{:S(2)}) copy-start(bf16[1,8,16,2048]{3,2,1,0:T(8,128)(2,1)} %param.10) | copy-start | bytes 1572868
  13.7 9.0 %copy-start.8 = (s32[1,8,16,4]{2,3,1,0:T(4,128)S(1)}, s32[1,8,16,4]{2,3,1,0:T(4,128)}, u32[]{:S(2)}) copy-start(s32[1,8,16,4]{2,3,1,0:T(4,128)} %param.12) | copy-start | bytes 6148
  13.7 9.7 %copy-start.9 = (bf16[2,16,2048]{2,1,0:T(8,128)(2,1)S(1)}, bf16[2,16,2048]{2,1,0:T(8,128)(2,1)}, u32[]{:S(2)}) copy-start(bf16[2,16,2048]{2,1,0:T(8,128)(2,1)} %param.11) | copy-start | bytes 393220
  13.7 61.3 %all-to-all-start.2 = ((bf16[8,8,9,2048]{3,0,2,1:T(8,128)(2,1)}), bf16[8,8,9,2048]{3,0,2,1:T(8,128)(2,1)S(1)}, u32[]{:S(2)}, u32[]{:S(2)}) async-start(bf16[8,8,9,2048]{3,0,2,1:T(8,128)(2,1)} %bitcast.100), calls=%async_computation.2 | async-start | bytes 4718592 | tf_op jit(solution)/shard_map/all_to_all | solution.py:79
  81.8 4.6 copy-start.2
  86.4 5.0 copy-start
  97.5 3.2 collective-permute-start
  103.8 19.2 %all-to-all-start = ((bf16[2,8,9,2048]{3,0,2,1:T(2,128)(2,1)}), bf16[2,8,9,2048]{3,0,2,1:T(2,128)(2,1)S(1)}, u32[]{:S(2)}, u32[]{:S(2)}) async-start(bf16[2,8,9,2048]{3,0,2,1:T(2,128)(2,1)} %bitcast.92), calls=%async_computation | async-start | bytes 1179648 | tf_op jit(solution)/shard_map/while/body/eval_jaxpr/all_to_all | solution.py:114
  127.1 3.9 copy-start.1
  136.6 22.2 %all-to-all-start.1 = ((bf16[2,8,9,2176]{3,0,2,1:T(2,128)(2,1)}), bf16[2,8,9,2176]{3,0,2,1:T(2,128)(2,1)S(1)}, u32[]{:S(2)}, u32[]{:S(2)}) async-start(bf16[2,8,9,2176]{3,0,2,1:T(2,128)(2,1)} %copy.62), calls=%async_computation.1 | async-start | bytes 1253376 | tf_op jit(solution)/shard_map/while/body/eval_jaxpr/all_to_all | solution.py:137
  164.4 3.2 collective-permute-start
  170.8 19.2 %all-to-all-start = ((bf16[2,8,9,2048]{3,0,2,1:T(2,128)(2,1)}), bf16[2,8,9,2048]{3,0,2,1:T(2,128)(2,1)S(1)}, u32[]{:S(2)}, u32[]{:S(2)}) async-start(bf16[2,8,9,2048]{3,0,2,1:T(2,128)(2,1)} %bitcast.92), calls=%async_computation | async-start | bytes 1179648 | tf_op jit(solution)/shard_map/while/body/eval_jaxpr/all_to_all | solution.py:114
  194.0 3.9 copy-start.1
  203.5 22.2 %all-to-all-start.1 = ((bf16[2,8,9,2176]{3,0,2,1:T(2,128)(2,1)}), bf16[2,8,9,2176]{3,0,2,1:T(2,128)(2,1)S(1)}, u32[]{:S(2)}, u32[]{:S(2)}) async-start(bf16[2,8,9,2176]{3,0,2,1:T(2,128)(2,1)} %copy.62), calls=%async_computation.1 | async-start | bytes 1253376 | tf_op jit(solution)/shard_map/while/body/eval_jaxpr/all_to_all | solution.py:137
  231.3 3.2 collective-permute-start
  237.7 19.2 %all-to-all-start = ((bf16[2,8,9,2048]{3,0,2,1:T(2,128)(2,1)}), bf16[2,8,9,2048]{3,0,2,1:T(2,128)(2,1)S(1)}, u32[]{:S(2)}, u32[]{:S(2)}) async-start(bf16[2,8,9,2048]{3,0,2,1:T(2,128)(2,1)} %bitcast.92), calls=%async_computation | async-start | bytes 1179648 | tf_op jit(solution)/shard_map/while/body/eval_jaxpr/all_to_all | solution.py:114
  260.9 3.9 copy-start.1
  270.5 22.2 %all-to-all-start.1 = ((bf16[2,8,9,2176]{3,0,2,1:T(2,128)(2,1)}), bf16[2,8,9,2176]{3,0,2,1:T(2,128)(2,1)S(1)}, u32[]{:S(2)}, u32[]{:S(2)}) async-start(bf16[2,8,9,2176]{3,0,2,1:T(2,128)(2,1)} %copy.62), calls=%async_computation.1 | async-start | bytes 1253376 | tf_op jit(solution)/shard_map/while/body/eval_jaxpr/all_to_all | solution.py:137
  298.2 3.2 collective-permute-start
  304.6 19.2 %all-to-all-start = ((bf16[2,8,9,2048]{3,0,2,1:T(2,128)(2,1)}), bf16[2,8,9,2048]{3,0,2,1:T(2,128)(2,1)S(1)}, u32[]{:S(2)}, u32[]{:S(2)}) async-start(bf16[2,8,9,2048]{3,0,2,1:T(2,128)(2,1)} %bitcast.92), calls=%async_computation | async-start | bytes 1179648 | tf_op jit(solution)/shard_map/while/body/eval_jaxpr/all_to_all | solution.py:114
  327.8 3.9 copy-start.1
  337.4 22.2 %all-to-all-start.1 = ((bf16[2,8,9,2176]{3,0,2,1:T(2,128)(2,1)}), bf16[2,8,9,2176]{3,0,2,1:T(2,128)(2,1)S(1)}, u32[]{:S(2)}, u32[]{:S(2)}) async-start(bf16[2,8,9,2176]{3,0,2,1:T(2,128)(2,1)} %copy.62), calls=%async_computation.1 | async-start | bytes 1253376 | tf_op jit(solution)/shard_map/while/body/eval_jaxpr/all_to_all | solution.py:137
  365.1 3.2 collective-permute-start
  371.5 19.2 %all-to-all-start = ((bf16[2,8,9,2048]{3,0,2,1:T(2,128)(2,1)}), bf16[2,8,9,2048]{3,0,2,1:T(2,128)(2,1)S(1)}, u32[]{:S(2)}, u32[]{:S(2)}) async-start(bf16[2,8,9,2048]{3,0,2,1:T(2,128)(2,1)} %bitcast.92), calls=%async_computation | async-start | bytes 1179648 | tf_op jit(solution)/shard_map/while/body/eval_jaxpr/all_to_all | solution.py:114
  394.7 3.9 copy-start.1
  404.3 22.2 %all-to-all-start.1 = ((bf16[2,8,9,2176]{3,0,2,1:T(2,128)(2,1)}), bf16[2,8,9,2176]{3,0,2,1:T(2,128)(2,1)S(1)}, u32[]{:S(2)}, u32[]{:S(2)}) async-start(bf16[2,8,9,2176]{3,0,2,1:T(2,128)(2,1)} %copy.62), calls=%async_computation.1 | async-start | bytes 1253376 | tf_op jit(solution)/shard_map/while/body/eval_jaxpr/all_to_all | solution.py:137
  432.1 3.2 collective-permute-start
  438.4 19.2 %all-to-all-start = ((bf16[2,8,9,2048]{3,0,2,1:T(2,128)(2,1)}), bf16[2,8,9,2048]{3,0,2,1:T(2,128)(2,1)S(1)}, u32[]{:S(2)}, u32[]{:S(2)}) async-start(bf16[2,8,9,2048]{3,0,2,1:T(2,128)(2,1)} %bitcast.92), calls=%async_computation | async-start | bytes 1179648 | tf_op jit(solution)/shard_map/while/body/eval_jaxpr/all_to_all | solution.py:114
  471.2 22.2 %all-to-all-start.1 = ((bf16[2,8,9,2176]{3,0,2,1:T(2,128)(2,1)}), bf16[2,8,9,2176]{3,0,2,1:T(2,128)(2,1)S(1)}, u32[]{:S(2)}, u32[]{:S(2)}) async-start(bf16[2,8,9,2176]{3,0,2,1:T(2,128)(2,1)} %copy.62), calls=%async_computation.1 | async-start | bytes 1253376 | tf_op jit(solution)/shard_map/while/body/eval_jaxpr/all_to_all | solution.py:137
  499.0 3.2 collective-permute-start
  505.3 19.2 %all-to-all-start = ((bf16[2,8,9,2048]{3,0,2,1:T(2,128)(2,1)}), bf16[2,8,9,2048]{3,0,2,1:T(2,128)(2,1)S(1)}, u32[]{:S(2)}, u32[]{:S(2)}) async-start(bf16[2,8,9,2048]{3,0,2,1:T(2,128)(2,1)} %bitcast.92), calls=%async_computation | async-start | bytes 1179648 | tf_op jit(solution)/shard_map/while/body/eval_jaxpr/all_to_all | solution.py:114
  538.1 22.2 %all-to-all-start.1 = ((bf16[2,8,9,2176]{3,0,2,1:T(2,128)(2,1)}), bf16[2,8,9,2176]{3,0,2,1:T(2,128)(2,1)S(1)}, u32[]{:S(2)}, u32[]{:S(2)}) async-start(bf16[2,8,9,2176]{3,0,2,1:T(2,128)(2,1)} %copy.62), calls=%async_computation.1 | async-start | bytes 1253376 | tf_op jit(solution)/shard_map/while/body/eval_jaxpr/all_to_all | solution.py:137
  (24 other events, 53.8 us)

commit v2 on v1

--- a/solution.py
+++ b/solution.py
@@ -83,9 +83,8 @@
     squash = jax.nn.sigmoid(gate)
     active = gate * squash
     hidden = (active * up_rows).astype(jnp.bfloat16)
-    output = jnp.dot(hidden, down_w, preferred_element_type=jnp.float32)
     factor = up_rows * squash * (1.0 + gate * (1.0 - squash))
-    output = output.reshape(micro, slots, width)
+    hidden = hidden.reshape(micro, slots, -1)
     factor = factor.reshape(micro, slots, -1)
     active = active.reshape(micro, slots, -1)
 
@@ -113,11 +112,11 @@
         )
         got_grad = lax.all_to_all(sent_grad, "expert", split_axis=1, concat_axis=1, tiled=True)
         rows_grad = got_grad.reshape(chunk * slots, width)
-        out_now = take(output, start).reshape(chunk * slots, width)
-        dprob = jnp.sum(out_now * rows_grad.astype(jnp.float32), axis=-1)
         dhidden = lax.dot_general(
             rows_grad, down_w, (((1,), (1,)), ((), ())), preferred_element_type=jnp.float32
         )
+        hidden_now = take(hidden, start).reshape(chunk * slots, -1)
+        dprob = jnp.sum(hidden_now.astype(jnp.float32) * dhidden, axis=-1)
         factor_now = take(factor, start).reshape(chunk * slots, -1)
         active_now = take(active, start).reshape(chunk * slots, -1)
         dgate = (dhidden * factor_now).astype(jnp.bfloat16)

time: 570 us -> 541 us (0.949)
  other arithmetic: 62.1 us -> 38.8 us
  waiting for transfers between devices: 269 us -> 262 us
    reduce_sum x7 -> x0, other arithmetic: 23.3 us -> none  [advance(): dprob = jnp.sum(out_now * rows_grad.astype(jnp.float32), axis=-1)]
    all_to_all x7, waiting for transfers between devices: 99.5 us -> 92.6 us  [advance(): lax.all_to_all(sent_grad, 'expert', split_axis=1, concat_axis=1, tiled=True)]
    dynamic_slice x21 -> x28, local copies, waits for them, and re-layouts: 14.7 us -> 21.6 us  [take(): return lax.dynamic_slice_in_dim(values, start, chunk, 0)]
  transfers between devices with their start and end apart: 22 -> 22, of which waited for: 22 -> 22; matrix products, arithmetic and copies ran while one was open for 3% -> 5% of each run, Pallas kernels for 0% -> 0%
where the time goes in v2:
time: 541 us; the launch traced here: 537 us
  waiting for transfers between devices  262 us (48%)
  starting transfers between devices  78 us (14%)
  matrix products  76.1 us (14%)
  local copies, waits for them, and re-layouts  73 us (13%)
  other arithmetic  38.8 us (7%)
  blocking collectives  7.61 us (1%)
    all_to_all x7, waiting for transfers between devices, advance(): lax.all_to_all(packed, 'expert', split_axis=1, concat_axis=1, tiled=True)  114 us
    all_to_all x7, waiting for transfers between devices, advance(): lax.all_to_all(sent_grad, 'expert', split_axis=1, concat_axis=1, tiled=True)  92.6 us
    all_to_all x1, waiting for transfers between devices, shards(): lax.all_to_all(sent_normed, 'expert', split_axis=1, concat_axis=1, tiled=...  42.1 us
    all_to_all x7, starting transfers between devices, advance(): lax.all_to_all(packed, 'expert', split_axis=1, concat_axis=1, tiled=True)  36.2 us
    dot_general x7, matrix products, advance(): lax.dot_general(rows_grad, down_w, (((1,), (1,)), ((), ())), preferred_el...  28.1 us
    all_to_all x7, starting transfers between devices, advance(): lax.all_to_all(sent_grad, 'expert', split_axis=1, concat_axis=1, tiled=True)  25.4 us
    dynamic_slice x28, local copies, waits for them, and re-layouts, take(): return lax.dynamic_slice_in_dim(values, start, chunk, 0)  21.6 us
    ppermute x7, waiting for transfers between devices, shifted(): return lax.ppermute(shard, axis, pairs)  13.5 us
  transfers between devices with their start and end apart: 22, of which 22 were waited for; matrix products, arithmetic and copies ran while one was open for 5% of the time, Pallas kernels for 0%

profile of v2, /device:TPU:0, one launch (start us, length us, event | category | flops | bytes accessed | tf_op | source)
XLA Modules:
  0.0 537.0 jit_solution(10226586049652227413)
XLA Ops:
  13.7 7.4 %all-to-all-start.2 = ((bf16[8,8,9,2048]{3,0,2,1:T(8,128)(2,1)}), bf16[8,8,9,2048]{3,0,2,1:T(8,128)(2,1)S(1)}, u32[]{:S(2)}, u32[]{:S(2)}) async-start(bf16[8,8,9,2048]{3,0,2,1:T(8,128)(2,1)} %bitcast.96), calls=%async_computation.2 | async-start | bytes 4718592 | tf_op jit(solution)/shard_map/all_to_all | solution.py:79
  23.4 7.6 %all_gather.3 = bf16[8,16,2048]{2,1,0:T(8,128)(2,1)} all-gather(bf16[2,16,2048]{2,1,0:T(8,128)(2,1)S(1)} %copy-done.8), channel_id=1, replica_groups=mesh['section'=4,'expert'=8] {'section'}, dimensions={0}, use_global_device_ids=true | all-gather | bytes 655360 | tf_op jit(solution)/shard_map/all_gather | solution.py:75
  32.9 42.1 %all-to-all-done.2 = bf16[8,8,9,2048]{3,0,2,1:T(8,128)(2,1)S(1)} async-done(((bf16[8,8,9,2048]{3,0,2,1:T(8,128)(2,1)}), bf16[8,8,9,2048]{3,0,2,1:T(8,128)(2,1)S(1)}, u32[]{:S(2)}, u32[]{:S(2)}) %all-to-all-start.2) | async-done | bytes 2359328 | tf_op jit(solution)/shard_map/all_to_all | solution.py:79
  81.8 4.5 fusion.35
  86.4 5.1 multiply_convert_fusion
  92.4 444.6 %while.18 = (s32[]{:T(128)}, bf16[2,16,2048]{2,1,0:T(8,128)(2,1)S(1)}, bf16[8,16,2048]{2,1,0:T(8,128)(2,1)}, pred[]{:T(512)}, s32[]{:T(128)}, /*index=5*/bf16[8,...) while((s32[]{:T(128)}, ...), condition=%wide.region_11.12_spmd.clone, body=%wide.region_5.11_spmd.clone.sunk | while | flops 1900805760 | bytes 83697488 | solution.py:163
  104.7 13.2 %all-to-all-done = bf16[2,8,9,2048]{3,0,2,1:T(2,128)(2,1)S(1)} async-done(((bf16[2,8,9,2048]{3,0,2,1:T(2,128)(2,1)}), bf16[2,8,9,2048]{3,0,2,1:T(2,128)(2,1)S(1)}, u32[]{:S(2)}, u32[]{:S(2)}) %all-to-all-start) | async-done | bytes 589856 | tf_op jit(solution)/shard_map/while/body/eval_jaxpr/all_to_all | solution.py:113
  118.4 4.0 fusion.82
  128.1 5.2 all-to-all-start.1
  134.1 16.3 %all-to-all-done.1 = bf16[2,8,9,2176]{3,0,2,1:T(2,128)(2,1)S(1)} async-done(((bf16[2,8,9,2176]{3,0,2,1:T(2,128)(2,1)}), bf16[2,8,9,2176]{3,0,2,1:T(2,128)(2,1)S(1)}, u32[]{:S(2)}, u32[]{:S(2)}) %all-to-all-start.1) | async-done | bytes 626720 | tf_op jit(solution)/shard_map/while/body/eval_jaxpr/all_to_all | solution.py:136
  168.2 13.2 %all-to-all-done = bf16[2,8,9,2048]{3,0,2,1:T(2,128)(2,1)S(1)} async-done(((bf16[2,8,9,2048]{3,0,2,1:T(2,128)(2,1)}), bf16[2,8,9,2048]{3,0,2,1:T(2,128)(2,1)S(1)}, u32[]{:S(2)}, u32[]{:S(2)}) %all-to-all-start) | async-done | bytes 589856 | tf_op jit(solution)/shard_map/while/body/eval_jaxpr/all_to_all | solution.py:113
  182.0 4.0 fusion.82
  191.6 5.2 all-to-all-start.1
  197.6 16.3 %all-to-all-done.1 = bf16[2,8,9,2176]{3,0,2,1:T(2,128)(2,1)S(1)} async-done(((bf16[2,8,9,2176]{3,0,2,1:T(2,128)(2,1)}), bf16[2,8,9,2176]{3,0,2,1:T(2,128)(2,1)S(1)}, u32[]{:S(2)}, u32[]{:S(2)}) %all-to-all-start.1) | async-done | bytes 626720 | tf_op jit(solution)/shard_map/while/body/eval_jaxpr/all_to_all | solution.py:136
  231.7 13.2 %all-to-all-done = bf16[2,8,9,2048]{3,0,2,1:T(2,128)(2,1)S(1)} async-done(((bf16[2,8,9,2048]{3,0,2,1:T(2,128)(2,1)}), bf16[2,8,9,2048]{3,0,2,1:T(2,128)(2,1)S(1)}, u32[]{:S(2)}, u32[]{:S(2)}) %all-to-all-start) | async-done | bytes 589856 | tf_op jit(solution)/shard_map/while/body/eval_jaxpr/all_to_all | solution.py:113
  245.5 4.0 fusion.82
  255.2 5.2 all-to-all-start.1
  261.1 16.3 %all-to-all-done.1 = bf16[2,8,9,2176]{3,0,2,1:T(2,128)(2,1)S(1)} async-done(((bf16[2,8,9,2176]{3,0,2,1:T(2,128)(2,1)}), bf16[2,8,9,2176]{3,0,2,1:T(2,128)(2,1)S(1)}, u32[]{:S(2)}, u32[]{:S(2)}) %all-to-all-start.1) | async-done | bytes 626720 | tf_op jit(solution)/shard_map/while/body/eval_jaxpr/all_to_all | solution.py:136
  295.2 13.2 %all-to-all-done = bf16[2,8,9,2048]{3,0,2,1:T(2,128)(2,1)S(1)} async-done(((bf16[2,8,9,2048]{3,0,2,1:T(2,128)(2,1)}), bf16[2,8,9,2048]{3,0,2,1:T(2,128)(2,1)S(1)}, u32[]{:S(2)}, u32[]{:S(2)}) %all-to-all-start) | async-done | bytes 589856 | tf_op jit(solution)/shard_map/while/body/eval_jaxpr/all_to_all | solution.py:113
  309.0 4.0 fusion.82
  318.7 5.2 all-to-all-start.1
  324.6 16.3 %all-to-all-done.1 = bf16[2,8,9,2176]{3,0,2,1:T(2,128)(2,1)S(1)} async-done(((bf16[2,8,9,2176]{3,0,2,1:T(2,128)(2,1)}), bf16[2,8,9,2176]{3,0,2,1:T(2,128)(2,1)S(1)}, u32[]{:S(2)}, u32[]{:S(2)}) %all-to-all-start.1) | async-done | bytes 626720 | tf_op jit(solution)/shard_map/while/body/eval_jaxpr/all_to_all | solution.py:136
  358.7 13.2 %all-to-all-done = bf16[2,8,9,2048]{3,0,2,1:T(2,128)(2,1)S(1)} async-done(((bf16[2,8,9,2048]{3,0,2,1:T(2,128)(2,1)}), bf16[2,8,9,2048]{3,0,2,1:T(2,128)(2,1)S(1)}, u32[]{:S(2)}, u32[]{:S(2)}) %all-to-all-start) | async-done | bytes 589856 | tf_op jit(solution)/shard_map/while/body/eval_jaxpr/all_to_all | solution.py:113
  372.5 4.0 fusion.82
  382.2 5.2 all-to-all-start.1
  388.1 16.3 %all-to-all-done.1 = bf16[2,8,9,2176]{3,0,2,1:T(2,128)(2,1)S(1)} async-done(((bf16[2,8,9,2176]{3,0,2,1:T(2,128)(2,1)}), bf16[2,8,9,2176]{3,0,2,1:T(2,128)(2,1)S(1)}, u32[]{:S(2)}, u32[]{:S(2)}) %all-to-all-start.1) | async-done | bytes 626720 | tf_op jit(solution)/shard_map/while/body/eval_jaxpr/all_to_all | solution.py:136
  422.3 13.2 %all-to-all-done = bf16[2,8,9,2048]{3,0,2,1:T(2,128)(2,1)S(1)} async-done(((bf16[2,8,9,2048]{3,0,2,1:T(2,128)(2,1)}), bf16[2,8,9,2048]{3,0,2,1:T(2,128)(2,1)S(1)}, u32[]{:S(2)}, u32[]{:S(2)}) %all-to-all-start) | async-done | bytes 589856 | tf_op jit(solution)/shard_map/while/body/eval_jaxpr/all_to_all | solution.py:113
  445.7 5.2 all-to-all-start.1
  451.7 16.3 %all-to-all-done.1 = bf16[2,8,9,2176]{3,0,2,1:T(2,128)(2,1)S(1)} async-done(((bf16[2,8,9,2176]{3,0,2,1:T(2,128)(2,1)}), bf16[2,8,9,2176]{3,0,2,1:T(2,128)(2,1)S(1)}, u32[]{:S(2)}, u32[]{:S(2)}) %all-to-all-start.1) | async-done | bytes 626720 | tf_op jit(solution)/shard_map/while/body/eval_jaxpr/all_to_all | solution.py:136
  485.8 13.2 %all-to-all-done = bf16[2,8,9,2048]{3,0,2,1:T(2,128)(2,1)S(1)} async-done(((bf16[2,8,9,2048]{3,0,2,1:T(2,128)(2,1)}), bf16[2,8,9,2048]{3,0,2,1:T(2,128)(2,1)S(1)}, u32[]{:S(2)}, u32[]{:S(2)}) %all-to-all-start) | async-done | bytes 589856 | tf_op jit(solution)/shard_map/while/body/eval_jaxpr/all_to_all | solution.py:113
  509.2 5.2 all-to-all-start.1
  515.2 16.3 %all-to-all-done.1 = bf16[2,8,9,2176]{3,0,2,1:T(2,128)(2,1)S(1)} async-done(((bf16[2,8,9,2176]{3,0,2,1:T(2,128)(2,1)}), bf16[2,8,9,2176]{3,0,2,1:T(2,128)(2,1)S(1)}, u32[]{:S(2)}, u32[]{:S(2)}) %all-to-all-start.1) | async-done | bytes 626720 | tf_op jit(solution)/shard_map/while/body/eval_jaxpr/all_to_all | solution.py:136
  (341 shorter events, 206.1 us)
Async XLA Ops:
  13.7 7.5 %copy-start.4 = (bf16[1,8,16,2048]{3,2,1,0:T(8,128)(2,1)S(1)}, bf16[1,8,16,2048]{3,2,1,0:T(8,128)(2,1)}, u32[]{:S(2)}) copy-start(bf16[1,8,16,2048]{3,2,1,0:T(8,128)(2,1)} %param.10) | copy-start | bytes 1572868
  13.7 9.0 %copy-start.7 = (s32[1,8,16,4]{2,3,1,0:T(4,128)S(1)}, s32[1,8,16,4]{2,3,1,0:T(4,128)}, u32[]{:S(2)}) copy-start(s32[1,8,16,4]{2,3,1,0:T(4,128)} %param.12) | copy-start | bytes 6148
  13.7 9.7 %copy-start.8 = (bf16[2,16,2048]{2,1,0:T(8,128)(2,1)S(1)}, bf16[2,16,2048]{2,1,0:T(8,128)(2,1)}, u32[]{:S(2)}) copy-start(bf16[2,16,2048]{2,1,0:T(8,128)(2,1)} %param.11) | copy-start | bytes 393220
  13.7 61.3 %all-to-all-start.2 = ((bf16[8,8,9,2048]{3,0,2,1:T(8,128)(2,1)}), bf16[8,8,9,2048]{3,0,2,1:T(8,128)(2,1)S(1)}, u32[]{:S(2)}, u32[]{:S(2)}) async-start(bf16[8,8,9,2048]{3,0,2,1:T(8,128)(2,1)} %bitcast.96), calls=%async_computation.2 | async-start | bytes 4718592 | tf_op jit(solution)/shard_map/all_to_all | solution.py:79
  81.8 4.6 copy-start.1
  92.4 3.2 collective-permute-start
  98.7 19.2 %all-to-all-start = ((bf16[2,8,9,2048]{3,0,2,1:T(2,128)(2,1)}), bf16[2,8,9,2048]{3,0,2,1:T(2,128)(2,1)S(1)}, u32[]{:S(2)}, u32[]{:S(2)}) async-start(bf16[2,8,9,2048]{3,0,2,1:T(2,128)(2,1)} %bitcast.89), calls=%async_computation | async-start | bytes 1179648 | tf_op jit(solution)/shard_map/while/body/eval_jaxpr/all_to_all | solution.py:113
  118.4 4.0 copy-start
  128.1 22.2 %all-to-all-start.1 = ((bf16[2,8,9,2176]{3,0,2,1:T(2,128)(2,1)}), bf16[2,8,9,2176]{3,0,2,1:T(2,128)(2,1)S(1)}, u32[]{:S(2)}, u32[]{:S(2)}) async-start(bf16[2,8,9,2176]{3,0,2,1:T(2,128)(2,1)} %copy.42), calls=%async_computation.1 | async-start | bytes 1253376 | tf_op jit(solution)/shard_map/while/body/eval_jaxpr/all_to_all | solution.py:136
  155.9 3.2 collective-permute-start
  162.2 19.2 %all-to-all-start = ((bf16[2,8,9,2048]{3,0,2,1:T(2,128)(2,1)}), bf16[2,8,9,2048]{3,0,2,1:T(2,128)(2,1)S(1)}, u32[]{:S(2)}, u32[]{:S(2)}) async-start(bf16[2,8,9,2048]{3,0,2,1:T(2,128)(2,1)} %bitcast.89), calls=%async_computation | async-start | bytes 1179648 | tf_op jit(solution)/shard_map/while/body/eval_jaxpr/all_to_all | solution.py:113
  181.9 4.0 copy-start
  191.6 22.2 %all-to-all-start.1 = ((bf16[2,8,9,2176]{3,0,2,1:T(2,128)(2,1)}), bf16[2,8,9,2176]{3,0,2,1:T(2,128)(2,1)S(1)}, u32[]{:S(2)}, u32[]{:S(2)}) async-start(bf16[2,8,9,2176]{3,0,2,1:T(2,128)(2,1)} %copy.42), calls=%async_computation.1 | async-start | bytes 1253376 | tf_op jit(solution)/shard_map/while/body/eval_jaxpr/all_to_all | solution.py:136
  219.4 3.2 collective-permute-start
  225.7 19.2 %all-to-all-start = ((bf16[2,8,9,2048]{3,0,2,1:T(2,128)(2,1)}), bf16[2,8,9,2048]{3,0,2,1:T(2,128)(2,1)S(1)}, u32[]{:S(2)}, u32[]{:S(2)}) async-start(bf16[2,8,9,2048]{3,0,2,1:T(2,128)(2,1)} %bitcast.89), calls=%async_computation | async-start | bytes 1179648 | tf_op jit(solution)/shard_map/while/body/eval_jaxpr/all_to_all | solution.py:113
  245.5 4.0 copy-start
  255.2 22.2 %all-to-all-start.1 = ((bf16[2,8,9,2176]{3,0,2,1:T(2,128)(2,1)}), bf16[2,8,9,2176]{3,0,2,1:T(2,128)(2,1)S(1)}, u32[]{:S(2)}, u32[]{:S(2)}) async-start(bf16[2,8,9,2176]{3,0,2,1:T(2,128)(2,1)} %copy.42), calls=%async_computation.1 | async-start | bytes 1253376 | tf_op jit(solution)/shard_map/while/body/eval_jaxpr/all_to_all | solution.py:136
  282.9 3.2 collective-permute-start
  289.3 19.2 %all-to-all-start = ((bf16[2,8,9,2048]{3,0,2,1:T(2,128)(2,1)}), bf16[2,8,9,2048]{3,0,2,1:T(2,128)(2,1)S(1)}, u32[]{:S(2)}, u32[]{:S(2)}) async-start(bf16[2,8,9,2048]{3,0,2,1:T(2,128)(2,1)} %bitcast.89), calls=%async_computation | async-start | bytes 1179648 | tf_op jit(solution)/shard_map/while/body/eval_jaxpr/all_to_all | solution.py:113
  309.0 4.0 copy-start
  318.7 22.2 %all-to-all-start.1 = ((bf16[2,8,9,2176]{3,0,2,1:T(2,128)(2,1)}), bf16[2,8,9,2176]{3,0,2,1:T(2,128)(2,1)S(1)}, u32[]{:S(2)}, u32[]{:S(2)}) async-start(bf16[2,8,9,2176]{3,0,2,1:T(2,128)(2,1)} %copy.42), calls=%async_computation.1 | async-start | bytes 1253376 | tf_op jit(solution)/shard_map/while/body/eval_jaxpr/all_to_all | solution.py:136
  346.5 3.2 collective-permute-start
  352.8 19.2 %all-to-all-start = ((bf16[2,8,9,2048]{3,0,2,1:T(2,128)(2,1)}), bf16[2,8,9,2048]{3,0,2,1:T(2,128)(2,1)S(1)}, u32[]{:S(2)}, u32[]{:S(2)}) async-start(bf16[2,8,9,2048]{3,0,2,1:T(2,128)(2,1)} %bitcast.89), calls=%async_computation | async-start | bytes 1179648 | tf_op jit(solution)/shard_map/while/body/eval_jaxpr/all_to_all | solution.py:113
  372.5 4.0 copy-start
  382.2 22.2 %all-to-all-start.1 = ((bf16[2,8,9,2176]{3,0,2,1:T(2,128)(2,1)}), bf16[2,8,9,2176]{3,0,2,1:T(2,128)(2,1)S(1)}, u32[]{:S(2)}, u32[]{:S(2)}) async-start(bf16[2,8,9,2176]{3,0,2,1:T(2,128)(2,1)} %copy.42), calls=%async_computation.1 | async-start | bytes 1253376 | tf_op jit(solution)/shard_map/while/body/eval_jaxpr/all_to_all | solution.py:136
  410.0 3.2 collective-permute-start
  416.3 19.2 %all-to-all-start = ((bf16[2,8,9,2048]{3,0,2,1:T(2,128)(2,1)}), bf16[2,8,9,2048]{3,0,2,1:T(2,128)(2,1)S(1)}, u32[]{:S(2)}, u32[]{:S(2)}) async-start(bf16[2,8,9,2048]{3,0,2,1:T(2,128)(2,1)} %bitcast.89), calls=%async_computation | async-start | bytes 1179648 | tf_op jit(solution)/shard_map/while/body/eval_jaxpr/all_to_all | solution.py:113
  436.0 4.0 copy-start
  445.7 22.2 %all-to-all-start.1 = ((bf16[2,8,9,2176]{3,0,2,1:T(2,128)(2,1)}), bf16[2,8,9,2176]{3,0,2,1:T(2,128)(2,1)S(1)}, u32[]{:S(2)}, u32[]{:S(2)}) async-start(bf16[2,8,9,2176]{3,0,2,1:T(2,128)(2,1)} %copy.42), calls=%async_computation.1 | async-start | bytes 1253376 | tf_op jit(solution)/shard_map/while/body/eval_jaxpr/all_to_all | solution.py:136
  473.5 3.2 collective-permute-start
  479.8 19.2 %all-to-all-start = ((bf16[2,8,9,2048]{3,0,2,1:T(2,128)(2,1)}), bf16[2,8,9,2048]{3,0,2,1:T(2,128)(2,1)S(1)}, u32[]{:S(2)}, u32[]{:S(2)}) async-start(bf16[2,8,9,2048]{3,0,2,1:T(2,128)(2,1)} %bitcast.89), calls=%async_computation | async-start | bytes 1179648 | tf_op jit(solution)/shard_map/while/body/eval_jaxpr/all_to_all | solution.py:113
  509.2 22.2 %all-to-all-start.1 = ((bf16[2,8,9,2176]{3,0,2,1:T(2,128)(2,1)}), bf16[2,8,9,2176]{3,0,2,1:T(2,128)(2,1)S(1)}, u32[]{:S(2)}, u32[]{:S(2)}) async-start(bf16[2,8,9,2176]{3,0,2,1:T(2,128)(2,1)} %copy.42), calls=%async_computation.1 | async-start | bytes 1253376 | tf_op jit(solution)/shard_map/while/body/eval_jaxpr/all_to_all | solution.py:136
  (23 other events, 50.1 us)

commit v3 on v2

--- a/solution.py
+++ b/solution.py
@@ -10,6 +10,13 @@
     devices = lax.axis_size(axis)
     pairs = [(i, i + by) for i in range(devices) if 0 <= i + by < devices]
     return lax.ppermute(shard, axis, pairs)
+
+
+def exchange(values):
+    shape = values.shape
+    folded = values.reshape(shape[:-1] + (shape[-1] // 128, 128))
+    folded = lax.all_to_all(folded, "expert", split_axis=1, concat_axis=1, tiled=True)
+    return folded.reshape(shape)
 
 
 def prepare(x_rows, gain):
@@ -76,7 +83,7 @@
 
     select = jax.vmap(lambda i: selection(i, experts, capacity))(ids)
     sent_normed = pack_rows(select, normed, per_token).reshape(micro, experts, capacity, width)
-    got_normed = lax.all_to_all(sent_normed, "expert", split_axis=1, concat_axis=1, tiled=True)
+    got_normed = exchange(sent_normed)
     rows = got_normed.reshape(micro * slots, width)
     gate = jnp.dot(rows, gate_w, preferred_element_type=jnp.float32)
     up_rows = jnp.dot(rows, up_w, preferred_element_type=jnp.float32)
@@ -110,7 +117,7 @@
         sent_grad = pack_rows(select_now, grad_in, per_token).reshape(
             chunk, experts, capacity, width
         )
-        got_grad = lax.all_to_all(sent_grad, "expert", split_axis=1, concat_axis=1, tiled=True)
+        got_grad = exchange(sent_grad)
         rows_grad = got_grad.reshape(chunk * slots, width)
         dhidden = lax.dot_general(
             rows_grad, down_w, (((1,), (1,)), ((), ())), preferred_element_type=jnp.float32
@@ -133,7 +140,7 @@
         extra = jnp.where(column == 0, high[:, None], jnp.where(column == 1, low[:, None], 0))
         packed = jnp.concatenate([returned.astype(jnp.bfloat16), extra.astype(jnp.bfloat16)], axis=1)
         packed = packed.reshape(chunk, experts, capacity, width + lanes)
-        back = lax.all_to_all(packed, "expert", split_axis=1, concat_axis=1, tiled=True)
+        back = exchange(packed)
         back = back.reshape(chunk, slots, width + lanes)
         pair = jnp.einsum("mps,msw->mpw", select_now, back, preferred_element_type=jnp.float32)
         pair_back = pair[..., :width].reshape(chunk, tok_rows, per_token, width)

time: 541 us -> 531 us (0.982)
  local copies, waits for them, and re-layouts: 73 us -> 61.6 us
  waiting for transfers between devices: 262 us -> 268 us
    convert_element_type x8 -> x0, local copies, waits for them, and re-layouts: 12.7 us -> none  [pack_rows(): return packed.astype(jnp.bfloat16)]
    all_to_all x15, waiting for transfers between devices: 248 us -> 254 us  [exchange(): lax.all_to_all(folded, 'expert', split_axis=1, concat_axis=1, tiled=True)]
    reshape x22 -> x28, local copies, waits for them, and re-layouts: 17.5 us -> 20.8 us  [the longest x21 18.7 us: exchange(): folded = values.reshape(shape[:-1] + (shape[-1] // 128, 128))]
  transfers between devices with their start and end apart: 22 -> 22, of which waited for: 22 -> 22; matrix products, arithmetic and copies ran while one was open for 5% -> 4% of each run, Pallas kernels for 0% -> 0%
where the time goes in v3:
time: 531 us; the launch traced here: 528 us
  waiting for transfers between devices  268 us (50%)
  starting transfers between devices  78 us (15%)
  matrix products  74.1 us (14%)
  local copies, waits for them, and re-layouts  61.6 us (12%)
  other arithmetic  37.2 us (7%)
  blocking collectives  7.6 us (1%)
    all_to_all x15, waiting for transfers between devices, exchange(): lax.all_to_all(folded, 'expert', split_axis=1, concat_axis=1, tiled=True)  254 us
    all_to_all x15, starting transfers between devices, exchange(): lax.all_to_all(folded, 'expert', split_axis=1, concat_axis=1, tiled=True)  68.9 us
    dot_general x7, matrix products, advance(): lax.dot_general(rows_grad, down_w, (((1,), (1,)), ((), ())), preferred_el...  28.1 us
    reshape x21, local copies, waits for them, and re-layouts, exchange(): folded = values.reshape(shape[:-1] + (shape[-1] // 128, 128))  18.7 us
    dynamic_slice x28, local copies, waits for them, and re-layouts, take(): return lax.dynamic_slice_in_dim(values, start, chunk, 0)  16.9 us
    ppermute x7, waiting for transfers between devices, shifted(): return lax.ppermute(shard, axis, pairs)  13.5 us
    dynamic_update_slice x7, other arithmetic, advance(): lax.dynamic_update_slice_in_dim(collected, jnp.where(working, result, ret...  12.1 us
    dot_general x7, matrix products, advance(): lax.dot_general(dgate, gate_w, (((1,), (1,)), ((), ())), preferred_elemen...  10.7 us
  transfers between devices with their start and end apart: 22, of which 22 were waited for; matrix products, arithmetic and copies ran while one was open for 4% of the time, Pallas kernels for 0%

profile of v3, /device:TPU:0, one launch (start us, length us, event | category | flops | bytes accessed | tf_op | source)
XLA Modules:
  0.0 527.8 jit_solution(1391771537978406342)
XLA Ops:
  13.6 7.4 %all-to-all-start.2 = ((bf16[8,8,9,16,128]{4,3,2,0,1:T(8,128)(2,1)}), bf16[8,8,9,16,128]{4,3,2,0,1:T(8,128)(2,1)}, u32[]{:S(2)}, u32[]{:S(2)}) async-start(bf16[8,8,9,16,128]{4,3,2,0,1:T(8,128)(2,1)} %copy.29), calls=%async_computation.2 | async-start | bytes 4718592 | tf_op jit(solution)/shard_map/all_to_all | solution.py:18
  23.2 7.6 %all_gather.3 = bf16[8,16,2048]{2,1,0:T(8,128)(2,1)} all-gather(bf16[2,16,2048]{2,1,0:T(8,128)(2,1)S(1)} %copy-done.8), channel_id=1, replica_groups=mesh['section'=4,'expert'=8] {'section'}, dimensions={0}, use_global_device_ids=true | all-gather | bytes 655360 | tf_op jit(solution)/shard_map/all_gather | solution.py:82
  31.7 43.3 %all-to-all-done.2 = bf16[8,8,9,16,128]{4,3,2,0,1:T(8,128)(2,1)} async-done(((bf16[8,8,9,16,128]{4,3,2,0,1:T(8,128)(2,1)}), bf16[8,8,9,16,128]{4,3,2,0,1:T(8,128)(2,1)}, u32[]{:S(2)}, u32[]{:S(2)}) %all-to-all-start.2) | async-done | bytes 2359328 | tf_op jit(solution)/shard_map/all_to_all | solution.py:18
  80.5 5.1 multiply_convert_fusion
  86.5 441.4 %while.18 = (s32[]{:T(128)}, bf16[2,16,2048]{2,1,0:T(8,128)(2,1)S(1)}, bf16[8,16,2048]{2,1,0:T(8,128)(2,1)}, pred[]{:T(512)}, s32[]{:T(128)}, /*index=5*/bf16[8,...) while((s32[]{:T(128)}, ...), condition=%wide.region_11.12_spmd.clone, body=%wide.region_5.11_spmd.clone.sunk | while | flops 1900805760 | bytes 82026352 | solution.py:170
  98.3 13.2 %all-to-all-done = bf16[2,8,9,16,128]{4,3,2,0,1:T(8,128)(2,1)S(1)} async-done(((bf16[2,8,9,16,128]{4,3,2,0,1:T(8,128)(2,1)}), bf16[2,8,9,16,128]{4,3,2,0,1:T(8,128)(2,1)S(1)}, u32[]{:S(2)}, u32[]{:S(2)}) %all-to-all-start) | async-done | bytes 589856 | tf_op jit(solution)/shard_map/while/body/eval_jaxpr/all_to_all | solution.py:18
  121.3 5.2 all-to-all-start.1
  126.6 16.9 %all-to-all-done.1 = bf16[2,8,9,17,128]{4,0,3,2,1:T(2,128)(2,1)S(1)} async-done(((bf16[2,8,9,17,128]{4,0,3,2,1:T(2,128)(2,1)}), bf16[2,8,9,17,128]{4,0,3,2,1:T(2,128)(2,1)S(1)}, u32[]{:S(2)}, u32[]{:S(2)}) %all-to-all-start.1) | async-done | bytes 626720 | tf_op jit(solution)/shard_map/while/body/eval_jaxpr/all_to_all | solution.py:18
  161.4 13.2 %all-to-all-done = bf16[2,8,9,16,128]{4,3,2,0,1:T(8,128)(2,1)S(1)} async-done(((bf16[2,8,9,16,128]{4,3,2,0,1:T(8,128)(2,1)}), bf16[2,8,9,16,128]{4,3,2,0,1:T(8,128)(2,1)S(1)}, u32[]{:S(2)}, u32[]{:S(2)}) %all-to-all-start) | async-done | bytes 589856 | tf_op jit(solution)/shard_map/while/body/eval_jaxpr/all_to_all | solution.py:18
  174.7 4.0 fusion.84
  184.4 5.2 all-to-all-start.1
  189.7 16.9 %all-to-all-done.1 = bf16[2,8,9,17,128]{4,0,3,2,1:T(2,128)(2,1)S(1)} async-done(((bf16[2,8,9,17,128]{4,0,3,2,1:T(2,128)(2,1)}), bf16[2,8,9,17,128]{4,0,3,2,1:T(2,128)(2,1)S(1)}, u32[]{:S(2)}, u32[]{:S(2)}) %all-to-all-start.1) | async-done | bytes 626720 | tf_op jit(solution)/shard_map/while/body/eval_jaxpr/all_to_all | solution.py:18
  224.4 13.2 %all-to-all-done = bf16[2,8,9,16,128]{4,3,2,0,1:T(8,128)(2,1)S(1)} async-done(((bf16[2,8,9,16,128]{4,3,2,0,1:T(8,128)(2,1)}), bf16[2,8,9,16,128]{4,3,2,0,1:T(8,128)(2,1)S(1)}, u32[]{:S(2)}, u32[]{:S(2)}) %all-to-all-start) | async-done | bytes 589856 | tf_op jit(solution)/shard_map/while/body/eval_jaxpr/all_to_all | solution.py:18
  237.7 4.0 fusion.84
  247.5 5.2 all-to-all-start.1
  252.7 16.9 %all-to-all-done.1 = bf16[2,8,9,17,128]{4,0,3,2,1:T(2,128)(2,1)S(1)} async-done(((bf16[2,8,9,17,128]{4,0,3,2,1:T(2,128)(2,1)}), bf16[2,8,9,17,128]{4,0,3,2,1:T(2,128)(2,1)S(1)}, u32[]{:S(2)}, u32[]{:S(2)}) %all-to-all-start.1) | async-done | bytes 626720 | tf_op jit(solution)/shard_map/while/body/eval_jaxpr/all_to_all | solution.py:18
  287.5 13.2 %all-to-all-done = bf16[2,8,9,16,128]{4,3,2,0,1:T(8,128)(2,1)S(1)} async-done(((bf16[2,8,9,16,128]{4,3,2,0,1:T(8,128)(2,1)}), bf16[2,8,9,16,128]{4,3,2,0,1:T(8,128)(2,1)S(1)}, u32[]{:S(2)}, u32[]{:S(2)}) %all-to-all-start) | async-done | bytes 589856 | tf_op jit(solution)/shard_map/while/body/eval_jaxpr/all_to_all | solution.py:18
  300.8 4.0 fusion.84
  310.5 5.2 all-to-all-start.1
  315.8 16.9 %all-to-all-done.1 = bf16[2,8,9,17,128]{4,0,3,2,1:T(2,128)(2,1)S(1)} async-done(((bf16[2,8,9,17,128]{4,0,3,2,1:T(2,128)(2,1)}), bf16[2,8,9,17,128]{4,0,3,2,1:T(2,128)(2,1)S(1)}, u32[]{:S(2)}, u32[]{:S(2)}) %all-to-all-start.1) | async-done | bytes 626720 | tf_op jit(solution)/shard_map/while/body/eval_jaxpr/all_to_all | solution.py:18
  350.5 13.2 %all-to-all-done = bf16[2,8,9,16,128]{4,3,2,0,1:T(8,128)(2,1)S(1)} async-done(((bf16[2,8,9,16,128]{4,3,2,0,1:T(8,128)(2,1)}), bf16[2,8,9,16,128]{4,3,2,0,1:T(8,128)(2,1)S(1)}, u32[]{:S(2)}, u32[]{:S(2)}) %all-to-all-start) | async-done | bytes 589856 | tf_op jit(solution)/shard_map/while/body/eval_jaxpr/all_to_all | solution.py:18
  363.8 4.0 fusion.84
  373.6 5.2 all-to-all-start.1
  378.8 16.9 %all-to-all-done.1 = bf16[2,8,9,17,128]{4,0,3,2,1:T(2,128)(2,1)S(1)} async-done(((bf16[2,8,9,17,128]{4,0,3,2,1:T(2,128)(2,1)}), bf16[2,8,9,17,128]{4,0,3,2,1:T(2,128)(2,1)S(1)}, u32[]{:S(2)}, u32[]{:S(2)}) %all-to-all-start.1) | async-done | bytes 626720 | tf_op jit(solution)/shard_map/while/body/eval_jaxpr/all_to_all | solution.py:18
  413.6 13.2 %all-to-all-done = bf16[2,8,9,16,128]{4,3,2,0,1:T(8,128)(2,1)S(1)} async-done(((bf16[2,8,9,16,128]{4,3,2,0,1:T(8,128)(2,1)}), bf16[2,8,9,16,128]{4,3,2,0,1:T(8,128)(2,1)S(1)}, u32[]{:S(2)}, u32[]{:S(2)}) %all-to-all-start) | async-done | bytes 589856 | tf_op jit(solution)/shard_map/while/body/eval_jaxpr/all_to_all | solution.py:18
  426.9 4.0 fusion.84
  436.6 5.2 all-to-all-start.1
  441.9 16.9 %all-to-all-done.1 = bf16[2,8,9,17,128]{4,0,3,2,1:T(2,128)(2,1)S(1)} async-done(((bf16[2,8,9,17,128]{4,0,3,2,1:T(2,128)(2,1)}), bf16[2,8,9,17,128]{4,0,3,2,1:T(2,128)(2,1)S(1)}, u32[]{:S(2)}, u32[]{:S(2)}) %all-to-all-start.1) | async-done | bytes 626720 | tf_op jit(solution)/shard_map/while/body/eval_jaxpr/all_to_all | solution.py:18
  476.6 13.2 %all-to-all-done = bf16[2,8,9,16,128]{4,3,2,0,1:T(8,128)(2,1)S(1)} async-done(((bf16[2,8,9,16,128]{4,3,2,0,1:T(8,128)(2,1)}), bf16[2,8,9,16,128]{4,3,2,0,1:T(8,128)(2,1)S(1)}, u32[]{:S(2)}, u32[]{:S(2)}) %all-to-all-start) | async-done | bytes 589856 | tf_op jit(solution)/shard_map/while/body/eval_jaxpr/all_to_all | solution.py:18
  489.9 4.0 fusion.84
  499.6 5.2 all-to-all-start.1
  504.9 16.9 %all-to-all-done.1 = bf16[2,8,9,17,128]{4,0,3,2,1:T(2,128)(2,1)S(1)} async-done(((bf16[2,8,9,17,128]{4,0,3,2,1:T(2,128)(2,1)}), bf16[2,8,9,17,128]{4,0,3,2,1:T(2,128)(2,1)S(1)}, u32[]{:S(2)}, u32[]{:S(2)}) %all-to-all-start.1) | async-done | bytes 626720 | tf_op jit(solution)/shard_map/while/body/eval_jaxpr/all_to_all | solution.py:18
  (371 shorter events, 191.6 us)
Async XLA Ops:
  13.6 7.5 %copy-start.4 = (bf16[1,8,16,2048]{3,2,1,0:T(8,128)(2,1)S(1)}, bf16[1,8,16,2048]{3,2,1,0:T(8,128)(2,1)}, u32[]{:S(2)}) copy-start(bf16[1,8,16,2048]{3,2,1,0:T(8,128)(2,1)} %param.10) | copy-start | bytes 1572868
  13.6 9.0 %copy-start.7 = (s32[1,8,16,4]{2,3,1,0:T(4,128)S(1)}, s32[1,8,16,4]{2,3,1,0:T(4,128)}, u32[]{:S(2)}) copy-start(s32[1,8,16,4]{2,3,1,0:T(4,128)} %param.12) | copy-start | bytes 6148
  13.6 9.6 %copy-start.8 = (bf16[2,16,2048]{2,1,0:T(8,128)(2,1)S(1)}, bf16[2,16,2048]{2,1,0:T(8,128)(2,1)}, u32[]{:S(2)}) copy-start(bf16[2,16,2048]{2,1,0:T(8,128)(2,1)} %param.11) | copy-start | bytes 393220
  13.6 61.4 %all-to-all-start.2 = ((bf16[8,8,9,16,128]{4,3,2,0,1:T(8,128)(2,1)}), bf16[8,8,9,16,128]{4,3,2,0,1:T(8,128)(2,1)}, u32[]{:S(2)}, u32[]{:S(2)}) async-start(bf16[8,8,9,16,128]{4,3,2,0,1:T(8,128)(2,1)} %copy.29), calls=%async_computation.2 | async-start | bytes 4718592 | tf_op jit(solution)/shard_map/all_to_all | solution.py:18
  86.5 40.1 %copy-start.9 = (f32[8,16,4]{1,2,0:T(4,128)}, f32[8,16,4]{1,2,0:T(4,128)S(1)}, u32[]{:S(2)}) copy-start(f32[8,16,4]{1,2,0:T(4,128)S(1)} %get-tuple-element.821) | copy-start | bytes 6148 | tf_op jit(solution)/shard_map/while
  86.5 3.2 collective-permute-start
  92.4 19.2 %all-to-all-start = ((bf16[2,8,9,16,128]{4,3,2,0,1:T(8,128)(2,1)}), bf16[2,8,9,16,128]{4,3,2,0,1:T(8,128)(2,1)S(1)}, u32[]{:S(2)}, u32[]{:S(2)}) async-start(bf16[2,8,9,16,128]{4,3,2,0,1:T(8,128)(2,1)} %copy.63), calls=%async_computation | async-start | bytes 1179648 | tf_op jit(solution)/shard_map/while/body/eval_jaxpr/all_to_all | solution.py:18
  121.3 22.2 %all-to-all-start.1 = ((bf16[2,8,9,17,128]{4,0,3,2,1:T(2,128)(2,1)}), bf16[2,8,9,17,128]{4,0,3,2,1:T(2,128)(2,1)S(1)}, u32[]{:S(2)}, u32[]{:S(2)}) async-start(bf16[2,8,9,17,128]{4,0,3,2,1:T(2,128)(2,1)} %copy.65), calls=%async_computation.1 | async-start | bytes 1253376 | tf_op jit(solution)/shard_map/while/body/eval_jaxpr/all_to_all | solution.py:18
  149.5 40.0 %copy-start.9 = (f32[8,16,4]{1,2,0:T(4,128)}, f32[8,16,4]{1,2,0:T(4,128)S(1)}, u32[]{:S(2)}) copy-start(f32[8,16,4]{1,2,0:T(4,128)S(1)} %get-tuple-element.821) | copy-start | bytes 6148 | tf_op jit(solution)/shard_map/while
  149.6 3.2 collective-permute-start
  155.4 19.2 %all-to-all-start = ((bf16[2,8,9,16,128]{4,3,2,0,1:T(8,128)(2,1)}), bf16[2,8,9,16,128]{4,3,2,0,1:T(8,128)(2,1)S(1)}, u32[]{:S(2)}, u32[]{:S(2)}) async-start(bf16[2,8,9,16,128]{4,3,2,0,1:T(8,128)(2,1)} %copy.63), calls=%async_computation | async-start | bytes 1179648 | tf_op jit(solution)/shard_map/while/body/eval_jaxpr/all_to_all | solution.py:18
  184.4 22.2 %all-to-all-start.1 = ((bf16[2,8,9,17,128]{4,0,3,2,1:T(2,128)(2,1)}), bf16[2,8,9,17,128]{4,0,3,2,1:T(2,128)(2,1)S(1)}, u32[]{:S(2)}, u32[]{:S(2)}) async-start(bf16[2,8,9,17,128]{4,0,3,2,1:T(2,128)(2,1)} %copy.65), calls=%async_computation.1 | async-start | bytes 1253376 | tf_op jit(solution)/shard_map/while/body/eval_jaxpr/all_to_all | solution.py:18
  212.6 40.0 %copy-start.9 = (f32[8,16,4]{1,2,0:T(4,128)}, f32[8,16,4]{1,2,0:T(4,128)S(1)}, u32[]{:S(2)}) copy-start(f32[8,16,4]{1,2,0:T(4,128)S(1)} %get-tuple-element.821) | copy-start | bytes 6148 | tf_op jit(solution)/shard_map/while
  212.6 3.2 collective-permute-start
  218.5 19.2 %all-to-all-start = ((bf16[2,8,9,16,128]{4,3,2,0,1:T(8,128)(2,1)}), bf16[2,8,9,16,128]{4,3,2,0,1:T(8,128)(2,1)S(1)}, u32[]{:S(2)}, u32[]{:S(2)}) async-start(bf16[2,8,9,16,128]{4,3,2,0,1:T(8,128)(2,1)} %copy.63), calls=%async_computation | async-start | bytes 1179648 | tf_op jit(solution)/shard_map/while/body/eval_jaxpr/all_to_all | solution.py:18
  247.5 22.2 %all-to-all-start.1 = ((bf16[2,8,9,17,128]{4,0,3,2,1:T(2,128)(2,1)}), bf16[2,8,9,17,128]{4,0,3,2,1:T(2,128)(2,1)S(1)}, u32[]{:S(2)}, u32[]{:S(2)}) async-start(bf16[2,8,9,17,128]{4,0,3,2,1:T(2,128)(2,1)} %copy.65), calls=%async_computation.1 | async-start | bytes 1253376 | tf_op jit(solution)/shard_map/while/body/eval_jaxpr/all_to_all | solution.py:18
  275.6 40.0 %copy-start.9 = (f32[8,16,4]{1,2,0:T(4,128)}, f32[8,16,4]{1,2,0:T(4,128)S(1)}, u32[]{:S(2)}) copy-start(f32[8,16,4]{1,2,0:T(4,128)S(1)} %get-tuple-element.821) | copy-start | bytes 6148 | tf_op jit(solution)/shard_map/while
  275.7 3.2 collective-permute-start
  281.5 19.2 %all-to-all-start = ((bf16[2,8,9,16,128]{4,3,2,0,1:T(8,128)(2,1)}), bf16[2,8,9,16,128]{4,3,2,0,1:T(8,128)(2,1)S(1)}, u32[]{:S(2)}, u32[]{:S(2)}) async-start(bf16[2,8,9,16,128]{4,3,2,0,1:T(8,128)(2,1)} %copy.63), calls=%async_computation | async-start | bytes 1179648 | tf_op jit(solution)/shard_map/while/body/eval_jaxpr/all_to_all | solution.py:18
  310.5 22.2 %all-to-all-start.1 = ((bf16[2,8,9,17,128]{4,0,3,2,1:T(2,128)(2,1)}), bf16[2,8,9,17,128]{4,0,3,2,1:T(2,128)(2,1)S(1)}, u32[]{:S(2)}, u32[]{:S(2)}) async-start(bf16[2,8,9,17,128]{4,0,3,2,1:T(2,128)(2,1)} %copy.65), calls=%async_computation.1 | async-start | bytes 1253376 | tf_op jit(solution)/shard_map/while/body/eval_jaxpr/all_to_all | solution.py:18
  338.7 40.0 %copy-start.9 = (f32[8,16,4]{1,2,0:T(4,128)}, f32[8,16,4]{1,2,0:T(4,128)S(1)}, u32[]{:S(2)}) copy-start(f32[8,16,4]{1,2,0:T(4,128)S(1)} %get-tuple-element.821) | copy-start | bytes 6148 | tf_op jit(solution)/shard_map/while
  338.7 3.2 collective-permute-start
  344.6 19.2 %all-to-all-start = ((bf16[2,8,9,16,128]{4,3,2,0,1:T(8,128)(2,1)}), bf16[2,8,9,16,128]{4,3,2,0,1:T(8,128)(2,1)S(1)}, u32[]{:S(2)}, u32[]{:S(2)}) async-start(bf16[2,8,9,16,128]{4,3,2,0,1:T(8,128)(2,1)} %copy.63), calls=%async_computation | async-start | bytes 1179648 | tf_op jit(solution)/shard_map/while/body/eval_jaxpr/all_to_all | solution.py:18
  373.6 22.2 %all-to-all-start.1 = ((bf16[2,8,9,17,128]{4,0,3,2,1:T(2,128)(2,1)}), bf16[2,8,9,17,128]{4,0,3,2,1:T(2,128)(2,1)S(1)}, u32[]{:S(2)}, u32[]{:S(2)}) async-start(bf16[2,8,9,17,128]{4,0,3,2,1:T(2,128)(2,1)} %copy.65), calls=%async_computation.1 | async-start | bytes 1253376 | tf_op jit(solution)/shard_map/while/body/eval_jaxpr/all_to_all | solution.py:18
  401.7 40.0 %copy-start.9 = (f32[8,16,4]{1,2,0:T(4,128)}, f32[8,16,4]{1,2,0:T(4,128)S(1)}, u32[]{:S(2)}) copy-start(f32[8,16,4]{1,2,0:T(4,128)S(1)} %get-tuple-element.821) | copy-start | bytes 6148 | tf_op jit(solution)/shard_map/while
  401.8 3.2 collective-permute-start
  407.6 19.2 %all-to-all-start = ((bf16[2,8,9,16,128]{4,3,2,0,1:T(8,128)(2,1)}), bf16[2,8,9,16,128]{4,3,2,0,1:T(8,128)(2,1)S(1)}, u32[]{:S(2)}, u32[]{:S(2)}) async-start(bf16[2,8,9,16,128]{4,3,2,0,1:T(8,128)(2,1)} %copy.63), calls=%async_computation | async-start | bytes 1179648 | tf_op jit(solution)/shard_map/while/body/eval_jaxpr/all_to_all | solution.py:18
  436.6 22.2 %all-to-all-start.1 = ((bf16[2,8,9,17,128]{4,0,3,2,1:T(2,128)(2,1)}), bf16[2,8,9,17,128]{4,0,3,2,1:T(2,128)(2,1)S(1)}, u32[]{:S(2)}, u32[]{:S(2)}) async-start(bf16[2,8,9,17,128]{4,0,3,2,1:T(2,128)(2,1)} %copy.65), calls=%async_computation.1 | async-start | bytes 1253376 | tf_op jit(solution)/shard_map/while/body/eval_jaxpr/all_to_all | solution.py:18
  464.8 40.0 %copy-start.9 = (f32[8,16,4]{1,2,0:T(4,128)}, f32[8,16,4]{1,2,0:T(4,128)S(1)}, u32[]{:S(2)}) copy-start(f32[8,16,4]{1,2,0:T(4,128)S(1)} %get-tuple-element.821) | copy-start | bytes 6148 | tf_op jit(solution)/shard_map/while
  464.8 3.2 collective-permute-start
  470.7 19.2 %all-to-all-start = ((bf16[2,8,9,16,128]{4,3,2,0,1:T(8,128)(2,1)}), bf16[2,8,9,16,128]{4,3,2,0,1:T(8,128)(2,1)S(1)}, u32[]{:S(2)}, u32[]{:S(2)}) async-start(bf16[2,8,9,16,128]{4,3,2,0,1:T(8,128)(2,1)} %copy.63), calls=%async_computation | async-start | bytes 1179648 | tf_op jit(solution)/shard_map/while/body/eval_jaxpr/all_to_all | solution.py:18
  499.6 22.2 %all-to-all-start.1 = ((bf16[2,8,9,17,128]{4,0,3,2,1:T(2,128)(2,1)}), bf16[2,8,9,17,128]{4,0,3,2,1:T(2,128)(2,1)S(1)}, u32[]{:S(2)}, u32[]{:S(2)}) async-start(bf16[2,8,9,17,128]{4,0,3,2,1:T(2,128)(2,1)} %copy.65), calls=%async_computation.1 | async-start | bytes 1253376 | tf_op jit(solution)/shard_map/while/body/eval_jaxpr/all_to_all | solution.py:18
  (31 other events, 97.3 us)

commit v4 on v3

--- a/solution.py
+++ b/solution.py
@@ -113,6 +113,19 @@
         working = jnp.logical_and(position >= 0, position < chunks)
         start = jnp.clip(position, 0, chunks - 1) * chunk
         grad_in = jnp.where(segment_index == segments - 1, take(top_full, start), arrived)
+        result = lax.cond(
+            working,
+            lambda operands: work(*operands),
+            lambda operands: jnp.zeros_like(operands[1]),
+            (start, grad_in),
+        )
+        retained = take(collected, start)
+        collected = lax.dynamic_update_slice_in_dim(
+            collected, jnp.where(working, result, retained), start, 0
+        )
+        return (result, collected)
+
+    def work(start, grad_in):
         select_now = take(select, start)
         sent_grad = pack_rows(select_now, grad_in, per_token).reshape(
             chunk, experts, capacity, width
@@ -157,11 +170,7 @@
             pair_back,
             pair_prob,
         )
-        retained = take(collected, start)
-        collected = lax.dynamic_update_slice_in_dim(
-            collected, jnp.where(working, result, retained), start, 0
-        )
-        return (result, collected)
+        return result
 
     begin = (
         jnp.zeros((chunk, tok_rows, width), jnp.bfloat16),

time: 531 us -> 494 us (0.930)
  starting transfers between devices: 78 us -> 49.4 us
  waiting for transfers between devices: 268 us -> 295 us
  matrix products: 74.1 us -> 47.4 us
  local copies, waits for them, and re-layouts: 61.6 us -> 50.7 us
    ppermute x7, waiting for transfers between devices: 13.5 us -> 172 us  [shifted(): return lax.ppermute(shard, axis, pairs)]
    all_to_all x15 -> x9, waiting for transfers between devices: 254 us -> 123 us  [exchange(): lax.all_to_all(folded, 'expert', split_axis=1, concat_axis=1, tiled=True)]
    all_to_all x15 -> x9, starting transfers between devices: 68.9 us -> 40.5 us  [exchange(): lax.all_to_all(folded, 'expert', split_axis=1, concat_axis=1, tiled=True)]
    dot_general x28 -> x16, matrix products: 51.5 us -> 29.5 us  [the longest x4 16.1 us: work(): lax.dot_general(rows_grad, down_w, (((1,), (1,)), ((), ())), preferred_el...]
    reshape x21 -> x12, local copies, waits for them, and re-layouts: 18.7 us -> 10.7 us  [exchange(): folded = values.reshape(shape[:-1] + (shape[-1] // 128, 128))]
    convert_element_type x1 -> x7, other arithmetic: 0.13 us -> 5.7 us  [selection(): (target[:, None] == jnp.arange(experts * capacity, dtype=jnp.int32)[None,...]
    while x77 -> x0, local copies, waits for them, and re-layouts: 5.45 us -> none
    reduce_sum x7 -> x4, other arithmetic: 5.41 us -> 0.06 us  [finish(): dfull = jnp.sum(pair_prob[..., None] * choose, axis=-2)]
  transfers between devices with their start and end apart: 22 -> 16, of which waited for: 22 -> 16; matrix products, arithmetic and copies ran while one was open for 4% -> 6% of each run, Pallas kernels for 0% -> 0%
where the time goes in v4:
time: 494 us; the launch traced here: 491 us
  waiting for transfers between devices  295 us (60%)
  local copies, waits for them, and re-layouts  50.7 us (10%)
  starting transfers between devices  49.4 us (10%)
  matrix products  47.4 us (10%)
  other arithmetic  39.5 us (8%)
  blocking collectives  7.61 us (2%)
    ppermute x7, waiting for transfers between devices, shifted(): return lax.ppermute(shard, axis, pairs)  172 us
    all_to_all x9, waiting for transfers between devices, exchange(): lax.all_to_all(folded, 'expert', split_axis=1, concat_axis=1, tiled=True)  123 us
    all_to_all x9, starting transfers between devices, exchange(): lax.all_to_all(folded, 'expert', split_axis=1, concat_axis=1, tiled=True)  40.5 us
    dot_general x4, matrix products, work(): lax.dot_general(rows_grad, down_w, (((1,), (1,)), ((), ())), preferred_el...  16.1 us
    dynamic_slice x12, local copies, waits for them, and re-layouts, take(): return lax.dynamic_slice_in_dim(values, start, chunk, 0)  12.1 us
    dynamic_update_slice x7, other arithmetic, advance(): lax.dynamic_update_slice_in_dim(collected, jnp.where(working, result, ret...  11.4 us
    reshape x12, local copies, waits for them, and re-layouts, exchange(): folded = values.reshape(shape[:-1] + (shape[-1] // 128, 128))  10.7 us
  transfers between devices with their start and end apart: 16, of which 16 were waited for; matrix products, arithmetic and copies ran while one was open for 6% of the time, Pallas kernels for 0%

profile of v4, /device:TPU:0, one launch (start us, length us, event | category | flops | bytes accessed | tf_op | source)
XLA Modules:
  0.0 491.1 jit_solution(7014408652329274939)
XLA Ops:
  14.8 7.4 %all-to-all-start.2 = ((bf16[8,8,9,16,128]{4,3,2,0,1:T(8,128)(2,1)}), bf16[8,8,9,16,128]{4,3,2,0,1:T(8,128)(2,1)}, u32[]{:S(2)}, u32[]{:S(2)}) async-start(bf16[8,8,9,16,128]{4,3,2,0,1:T(8,128)(2,1)} %copy.49), calls=%async_computation.2 | async-start | bytes 4718592 | tf_op jit(solution)/shard_map/all_to_all | solution.py:18
  25.3 7.6 %all_gather.3 = bf16[8,16,2048]{2,1,0:T(8,128)(2,1)} all-gather(bf16[2,16,2048]{2,1,0:T(8,128)(2,1)S(1)} %copy-done.9), channel_id=1, replica_groups=mesh['section'=4,'expert'=8] {'section'}, dimensions={0}, use_global_device_ids=true | all-gather | bytes 655360 | tf_op jit(solution)/shard_map/all_gather | solution.py:82
  33.0 43.1 %all-to-all-done.2 = bf16[8,8,9,16,128]{4,3,2,0,1:T(8,128)(2,1)} async-done(((bf16[8,8,9,16,128]{4,3,2,0,1:T(8,128)(2,1)}), bf16[8,8,9,16,128]{4,3,2,0,1:T(8,128)(2,1)}, u32[]{:S(2)}, u32[]{:S(2)}) %all-to-all-start.2) | async-done | bytes 2359328 | tf_op jit(solution)/shard_map/all_to_all | solution.py:18
  81.7 5.1 %multiply_convert_fusion = (bf16[576,1024]{1,0:T(8,128)(2,1)}, f32[576,1024]{1,0:T(8,128)}, f32[576,1024]{1,0:T(8,128)}) fusion(f32[576,1024]{1,0:T(8,128)S(1)} %fusion.27, bf16[1,1,2048,1024]{3,2,1,0:T(8,128)(2,1)S(1)} %copy-done.2, bf16[72,8,16,128]{3,2,1,0:T(8,128)(2,1)S(1)} %bitcast.96), kind=kOutput, calls=%fused_computation.57 | convolution fusion | flops 2422407168 | bytes 14811136 | tf_op jit(solution)/shard_map/dot_general | solution.py:89
  88.3 402.8 %while.18 = (s32[]{:T(128)}, bf16[2,16,2048]{2,1,0:T(8,128)(2,1)}, bf16[8,16,2048]{2,1,0:T(8,128)(2,1)}, s32[]{:T(128)}, pred[]{:T(512)}, /*index=5*/bf16[8,16,2...) while((s32[]{:T(128)}, bf16[2,16,2048]{2,1,0:T(8,128)(2,1)}, ...), condition=%wide.region_13.14_spmd.clone, body=%wide.region_5.13_spmd.clone.sunk | while | flops 1900822144 | bytes 82006056 | solution.py:179
  105.0 3.6 collective-permute-done
  113.8 140.5 %collective-permute-done = bf16[2,16,2048]{2,1,0:T(8,128)(2,1)S(1)} collective-permute-done((bf16[2,16,2048]{2,1,0:T(8,128)(2,1)}, bf16[2,16,2048]{2,1,0:T(8,128)(2,1)S(1)}, u32[]{:S(2)}, u32[]{:S(2)}) %collective-permute-start) | collective-permute-done | bytes 131104 | tf_op jit(solution)/shard_map/while/body/eval_jaxpr/ppermute | solution.py:12
  254.2 46.5 %conditional.3 = (bf16[2,16,2048]{2,1,0:T(8,128)(2,1)}) conditional(s32[]{:T(128)} %convert_element_type.171, () %tuple.61, (pred[]{:T(512)}, bf16[8,16,2048]{2,1,0:T(8,128)(2,1)}, s32[]{:T(128)}, bf16[2,16,2048]{2,1,0:T(8,128)(2,1)S(1)}, s32[]{:T(128)}, /*index=5*/f32[8,16,1]{1,0,2:T(8,128)}, f32[2048]{0:T(1024)}, f32[8,16,4]{2,1,0:T(8,128)}, ...), branch_computations={%region_6.6_spmd, %region_7.12_spmd} | conditional | flops 1900674688 | bytes 80993304 | solution.py:116
  256.9 3.7 all-to-all-start
  262.8 8.7 %all-to-all-done = bf16[2,8,9,16,128]{4,3,2,0,1:T(8,128)(2,1)S(1)} async-done(((bf16[2,8,9,16,128]{4,3,2,0,1:T(8,128)(2,1)}), bf16[2,8,9,16,128]{4,3,2,0,1:T(8,128)(2,1)S(1)}, u32[]{:S(2)}, u32[]{:S(2)}) %all-to-all-start) | async-done | bytes 589856 | tf_op jit(solution)/shard_map/while/body/eval_jaxpr/cond/branch_1_fun/all_to_all | solution.py:18
  271.6 4.0 fusion.10
  281.3 3.7 all-to-all-start.1
  286.9 9.4 %all-to-all-done.1 = bf16[2,8,9,17,128]{4,0,3,2,1:T(2,128)(2,1)S(1)} async-done(((bf16[2,8,9,17,128]{4,0,3,2,1:T(2,128)(2,1)}), bf16[2,8,9,17,128]{4,0,3,2,1:T(2,128)(2,1)S(1)}, u32[]{:S(2)}, u32[]{:S(2)}) %all-to-all-start.1) | async-done | bytes 626720 | tf_op jit(solution)/shard_map/while/body/eval_jaxpr/cond/branch_1_fun/all_to_all | solution.py:18
  305.2 11.9 %collective-permute-done = bf16[2,16,2048]{2,1,0:T(8,128)(2,1)S(1)} collective-permute-done((bf16[2,16,2048]{2,1,0:T(8,128)(2,1)}, bf16[2,16,2048]{2,1,0:T(8,128)(2,1)S(1)}, u32[]{:S(2)}, u32[]{:S(2)}) %collective-permute-start) | collective-permute-done | bytes 131104 | tf_op jit(solution)/shard_map/while/body/eval_jaxpr/ppermute | solution.py:12
  317.1 46.5 %conditional.3 = (bf16[2,16,2048]{2,1,0:T(8,128)(2,1)}) conditional(s32[]{:T(128)} %convert_element_type.171, () %tuple.61, (pred[]{:T(512)}, bf16[8,16,2048]{2,1,0:T(8,128)(2,1)}, s32[]{:T(128)}, bf16[2,16,2048]{2,1,0:T(8,128)(2,1)S(1)}, s32[]{:T(128)}, /*index=5*/f32[8,16,1]{1,0,2:T(8,128)}, f32[2048]{0:T(1024)}, f32[8,16,4]{2,1,0:T(8,128)}, ...), branch_computations={%region_6.6_spmd, %region_7.12_spmd} | conditional | flops 1900674688 | bytes 80993304 | solution.py:116
  319.8 3.7 all-to-all-start
  325.7 8.7 %all-to-all-done = bf16[2,8,9,16,128]{4,3,2,0,1:T(8,128)(2,1)S(1)} async-done(((bf16[2,8,9,16,128]{4,3,2,0,1:T(8,128)(2,1)}), bf16[2,8,9,16,128]{4,3,2,0,1:T(8,128)(2,1)S(1)}, u32[]{:S(2)}, u32[]{:S(2)}) %all-to-all-start) | async-done | bytes 589856 | tf_op jit(solution)/shard_map/while/body/eval_jaxpr/cond/branch_1_fun/all_to_all | solution.py:18
  334.5 4.0 fusion.10
  344.2 3.7 all-to-all-start.1
  349.9 9.4 %all-to-all-done.1 = bf16[2,8,9,17,128]{4,0,3,2,1:T(2,128)(2,1)S(1)} async-done(((bf16[2,8,9,17,128]{4,0,3,2,1:T(2,128)(2,1)}), bf16[2,8,9,17,128]{4,0,3,2,1:T(2,128)(2,1)S(1)}, u32[]{:S(2)}, u32[]{:S(2)}) %all-to-all-start.1) | async-done | bytes 626720 | tf_op jit(solution)/shard_map/while/body/eval_jaxpr/cond/branch_1_fun/all_to_all | solution.py:18
  368.1 11.6 %collective-permute-done = bf16[2,16,2048]{2,1,0:T(8,128)(2,1)S(1)} collective-permute-done((bf16[2,16,2048]{2,1,0:T(8,128)(2,1)}, bf16[2,16,2048]{2,1,0:T(8,128)(2,1)S(1)}, u32[]{:S(2)}, u32[]{:S(2)}) %collective-permute-start) | collective-permute-done | bytes 131104 | tf_op jit(solution)/shard_map/while/body/eval_jaxpr/ppermute | solution.py:12
  379.7 58.2 %conditional.3 = (bf16[2,16,2048]{2,1,0:T(8,128)(2,1)}) conditional(s32[]{:T(128)} %convert_element_type.171, () %tuple.61, (pred[]{:T(512)}, bf16[8,16,2048]{2,1,0:T(8,128)(2,1)}, s32[]{:T(128)}, bf16[2,16,2048]{2,1,0:T(8,128)(2,1)S(1)}, s32[]{:T(128)}, /*index=5*/f32[8,16,1]{1,0,2:T(8,128)}, f32[2048]{0:T(1024)}, f32[8,16,4]{2,1,0:T(8,128)}, ...), branch_computations={%region_6.6_spmd, %region_7.12_spmd} | conditional | flops 1900674688 | bytes 80993304 | solution.py:116
  382.4 3.7 all-to-all-start
  388.4 10.4 %all-to-all-done = bf16[2,8,9,16,128]{4,3,2,0,1:T(8,128)(2,1)S(1)} async-done(((bf16[2,8,9,16,128]{4,3,2,0,1:T(8,128)(2,1)}), bf16[2,8,9,16,128]{4,3,2,0,1:T(8,128)(2,1)S(1)}, u32[]{:S(2)}, u32[]{:S(2)}) %all-to-all-start) | async-done | bytes 589856 | tf_op jit(solution)/shard_map/while/body/eval_jaxpr/cond/branch_1_fun/all_to_all | solution.py:18
  398.8 4.0 fusion.10
  408.5 7.4 %all-to-all-start.1 = ((bf16[2,8,9,17,128]{4,0,3,2,1:T(2,128)(2,1)}), bf16[2,8,9,17,128]{4,0,3,2,1:T(2,128)(2,1)S(1)}, u32[]{:S(2)}, u32[]{:S(2)}) async-start(bf16[2,8,9,17,128]{4,0,3,2,1:T(2,128)(2,1)} %copy.44), calls=%async_computation.1 | async-start | bytes 1253376 | tf_op jit(solution)/shard_map/while/body/eval_jaxpr/cond/branch_1_fun/all_to_all | solution.py:18
  417.9 15.7 %all-to-all-done.1 = bf16[2,8,9,17,128]{4,0,3,2,1:T(2,128)(2,1)S(1)} async-done(((bf16[2,8,9,17,128]{4,0,3,2,1:T(2,128)(2,1)}), bf16[2,8,9,17,128]{4,0,3,2,1:T(2,128)(2,1)S(1)}, u32[]{:S(2)}, u32[]{:S(2)}) %all-to-all-start.1) | async-done | bytes 626720 | tf_op jit(solution)/shard_map/while/body/eval_jaxpr/cond/branch_1_fun/all_to_all | solution.py:18
  443.0 46.4 %conditional.3 = (bf16[2,16,2048]{2,1,0:T(8,128)(2,1)}) conditional(s32[]{:T(128)} %convert_element_type.171, () %tuple.61, (pred[]{:T(512)}, bf16[8,16,2048]{2,1,0:T(8,128)(2,1)}, s32[]{:T(128)}, bf16[2,16,2048]{2,1,0:T(8,128)(2,1)S(1)}, s32[]{:T(128)}, /*index=5*/f32[8,16,1]{1,0,2:T(8,128)}, f32[2048]{0:T(1024)}, f32[8,16,4]{2,1,0:T(8,128)}, ...), branch_computations={%region_6.6_spmd, %region_7.12_spmd} | conditional | flops 1900674688 | bytes 80993304 | solution.py:116
  451.6 8.7 %all-to-all-done = bf16[2,8,9,16,128]{4,3,2,0,1:T(8,128)(2,1)S(1)} async-done(((bf16[2,8,9,16,128]{4,3,2,0,1:T(8,128)(2,1)}), bf16[2,8,9,16,128]{4,3,2,0,1:T(8,128)(2,1)S(1)}, u32[]{:S(2)}, u32[]{:S(2)}) %all-to-all-start) | async-done | bytes 589856 | tf_op jit(solution)/shard_map/while/body/eval_jaxpr/cond/branch_1_fun/all_to_all | solution.py:18
  460.3 4.0 fusion.10
  470.0 3.7 all-to-all-start.1
  475.7 9.4 %all-to-all-done.1 = bf16[2,8,9,17,128]{4,0,3,2,1:T(2,128)(2,1)S(1)} async-done(((bf16[2,8,9,17,128]{4,0,3,2,1:T(2,128)(2,1)}), bf16[2,8,9,17,128]{4,0,3,2,1:T(2,128)(2,1)S(1)}, u32[]{:S(2)}, u32[]{:S(2)}) %all-to-all-start.1) | async-done | bytes 626720 | tf_op jit(solution)/shard_map/while/body/eval_jaxpr/cond/branch_1_fun/all_to_all | solution.py:18
  (243 shorter events, 135.2 us)
Async XLA Ops:
  2.5 19.7 %copy-start.5 = (f32[1,2048]{1,0:T(1,128)}, f32[1,2048]{1,0:T(1,128)S(1)}, u32[]{:S(2)}) copy-start(f32[1,2048]{1,0:T(1,128)S(1)} %convert_element_type.117) | copy-start | bytes 24580
  14.8 7.5 %copy-start.4 = (bf16[1,8,16,2048]{3,2,1,0:T(8,128)(2,1)S(1)}, bf16[1,8,16,2048]{3,2,1,0:T(8,128)(2,1)}, u32[]{:S(2)}) copy-start(bf16[1,8,16,2048]{3,2,1,0:T(8,128)(2,1)} %param.12) | copy-start | bytes 1572868
  14.8 10.6 %copy-start.9 = (bf16[2,16,2048]{2,1,0:T(8,128)(2,1)S(1)}, bf16[2,16,2048]{2,1,0:T(8,128)(2,1)}, u32[]{:S(2)}) copy-start(bf16[2,16,2048]{2,1,0:T(8,128)(2,1)} %param.13) | copy-start | bytes 393220
  14.8 61.4 %all-to-all-start.2 = ((bf16[8,8,9,16,128]{4,3,2,0,1:T(8,128)(2,1)}), bf16[8,8,9,16,128]{4,3,2,0,1:T(8,128)(2,1)}, u32[]{:S(2)}, u32[]{:S(2)}) async-start(bf16[8,8,9,16,128]{4,3,2,0,1:T(8,128)(2,1)} %copy.49), calls=%async_computation.2 | async-start | bytes 4718592 | tf_op jit(solution)/shard_map/all_to_all | solution.py:18
  76.2 2.9 copy-start
  79.1 2.6 copy-start.2
  88.3 3.4 collective-permute-start
  94.0 5.9 %collective-permute-start = (bf16[2,16,2048]{2,1,0:T(8,128)(2,1)}, bf16[2,16,2048]{2,1,0:T(8,128)(2,1)S(1)}, u32[]{:S(2)}, u32[]{:S(2)}) collective-permute-start(bf16[2,16,2048]{2,1,0:T(8,128)(2,1)} %get-tuple-element.832), channel_id=1, source_target_pairs={{8,0},{16,8},{24,16},{9,1},{17,9},{25,17},{10,2},{18,10},{26,18},{... | collective-permute-start | bytes 393224 | tf_op jit(solution)/shard_map/while/body/eval_jaxpr/ppermute | solution.py:12
  102.1 6.5 %collective-permute-start = (bf16[2,16,2048]{2,1,0:T(8,128)(2,1)}, bf16[2,16,2048]{2,1,0:T(8,128)(2,1)S(1)}, u32[]{:S(2)}, u32[]{:S(2)}) collective-permute-start(bf16[2,16,2048]{2,1,0:T(8,128)(2,1)} %get-tuple-element.832), channel_id=1, source_target_pairs={{8,0},{16,8},{24,16},{9,1},{17,9},{25,17},{10,2},{18,10},{26,18},{... | collective-permute-start | bytes 393224 | tf_op jit(solution)/shard_map/while/body/eval_jaxpr/ppermute | solution.py:12
  110.9 143.3 %collective-permute-start = (bf16[2,16,2048]{2,1,0:T(8,128)(2,1)}, bf16[2,16,2048]{2,1,0:T(8,128)(2,1)S(1)}, u32[]{:S(2)}, u32[]{:S(2)}) collective-permute-start(bf16[2,16,2048]{2,1,0:T(8,128)(2,1)} %get-tuple-element.832), channel_id=1, source_target_pairs={{8,0},{16,8},{24,16},{9,1},{17,9},{25,17},{10,2},{18,10},{26,18},{... | collective-permute-start | bytes 393224 | tf_op jit(solution)/shard_map/while/body/eval_jaxpr/ppermute | solution.py:12
  256.9 14.6 %all-to-all-start = ((bf16[2,8,9,16,128]{4,3,2,0,1:T(8,128)(2,1)}), bf16[2,8,9,16,128]{4,3,2,0,1:T(8,128)(2,1)S(1)}, u32[]{:S(2)}, u32[]{:S(2)}) async-start(bf16[2,8,9,16,128]{4,3,2,0,1:T(8,128)(2,1)} %copy.42), calls=%async_computation | async-start | bytes 1179648 | tf_op jit(solution)/shard_map/while/body/eval_jaxpr/cond/branch_1_fun/all_to_all | solution.py:18
  271.5 4.0 copy-start.1
  275.6 2.2 copy-start.3
  281.3 15.1 %all-to-all-start.1 = ((bf16[2,8,9,17,128]{4,0,3,2,1:T(2,128)(2,1)}), bf16[2,8,9,17,128]{4,0,3,2,1:T(2,128)(2,1)S(1)}, u32[]{:S(2)}, u32[]{:S(2)}) async-start(bf16[2,8,9,17,128]{4,0,3,2,1:T(2,128)(2,1)} %copy.44), calls=%async_computation.1 | async-start | bytes 1253376 | tf_op jit(solution)/shard_map/while/body/eval_jaxpr/cond/branch_1_fun/all_to_all | solution.py:18
  297.4 2.5 copy-start.10
  302.3 14.8 %collective-permute-start = (bf16[2,16,2048]{2,1,0:T(8,128)(2,1)}, bf16[2,16,2048]{2,1,0:T(8,128)(2,1)S(1)}, u32[]{:S(2)}, u32[]{:S(2)}) collective-permute-start(bf16[2,16,2048]{2,1,0:T(8,128)(2,1)} %get-tuple-element.832), channel_id=1, source_target_pairs={{8,0},{16,8},{24,16},{9,1},{17,9},{25,17},{10,2},{18,10},{26,18},{... | collective-permute-start | bytes 393224 | tf_op jit(solution)/shard_map/while/body/eval_jaxpr/ppermute | solution.py:12
  319.8 14.6 %all-to-all-start = ((bf16[2,8,9,16,128]{4,3,2,0,1:T(8,128)(2,1)}), bf16[2,8,9,16,128]{4,3,2,0,1:T(8,128)(2,1)S(1)}, u32[]{:S(2)}, u32[]{:S(2)}) async-start(bf16[2,8,9,16,128]{4,3,2,0,1:T(8,128)(2,1)} %copy.42), calls=%async_computation | async-start | bytes 1179648 | tf_op jit(solution)/shard_map/while/body/eval_jaxpr/cond/branch_1_fun/all_to_all | solution.py:18
  334.4 4.0 copy-start.1
  338.5 2.2 copy-start.3
  344.2 15.1 %all-to-all-start.1 = ((bf16[2,8,9,17,128]{4,0,3,2,1:T(2,128)(2,1)}), bf16[2,8,9,17,128]{4,0,3,2,1:T(2,128)(2,1)S(1)}, u32[]{:S(2)}, u32[]{:S(2)}) async-start(bf16[2,8,9,17,128]{4,0,3,2,1:T(2,128)(2,1)} %copy.44), calls=%async_computation.1 | async-start | bytes 1253376 | tf_op jit(solution)/shard_map/while/body/eval_jaxpr/cond/branch_1_fun/all_to_all | solution.py:18
  360.3 2.5 copy-start.10
  365.2 14.5 %collective-permute-start = (bf16[2,16,2048]{2,1,0:T(8,128)(2,1)}, bf16[2,16,2048]{2,1,0:T(8,128)(2,1)S(1)}, u32[]{:S(2)}, u32[]{:S(2)}) collective-permute-start(bf16[2,16,2048]{2,1,0:T(8,128)(2,1)} %get-tuple-element.832), channel_id=1, source_target_pairs={{8,0},{16,8},{24,16},{9,1},{17,9},{25,17},{10,2},{18,10},{26,18},{... | collective-permute-start | bytes 393224 | tf_op jit(solution)/shard_map/while/body/eval_jaxpr/ppermute | solution.py:12
  382.4 16.4 %all-to-all-start = ((bf16[2,8,9,16,128]{4,3,2,0,1:T(8,128)(2,1)}), bf16[2,8,9,16,128]{4,3,2,0,1:T(8,128)(2,1)S(1)}, u32[]{:S(2)}, u32[]{:S(2)}) async-start(bf16[2,8,9,16,128]{4,3,2,0,1:T(8,128)(2,1)} %copy.42), calls=%async_computation | async-start | bytes 1179648 | tf_op jit(solution)/shard_map/while/body/eval_jaxpr/cond/branch_1_fun/all_to_all | solution.py:18
  398.8 4.0 copy-start.1
  402.8 2.2 copy-start.3
  408.5 25.1 %all-to-all-start.1 = ((bf16[2,8,9,17,128]{4,0,3,2,1:T(2,128)(2,1)}), bf16[2,8,9,17,128]{4,0,3,2,1:T(2,128)(2,1)S(1)}, u32[]{:S(2)}, u32[]{:S(2)}) async-start(bf16[2,8,9,17,128]{4,0,3,2,1:T(2,128)(2,1)} %copy.44), calls=%async_computation.1 | async-start | bytes 1253376 | tf_op jit(solution)/shard_map/while/body/eval_jaxpr/cond/branch_1_fun/all_to_all | solution.py:18
  434.6 2.5 copy-start.10
  439.6 3.4 collective-permute-start
  445.6 14.6 %all-to-all-start = ((bf16[2,8,9,16,128]{4,3,2,0,1:T(8,128)(2,1)}), bf16[2,8,9,16,128]{4,3,2,0,1:T(8,128)(2,1)S(1)}, u32[]{:S(2)}, u32[]{:S(2)}) async-start(bf16[2,8,9,16,128]{4,3,2,0,1:T(8,128)(2,1)} %copy.42), calls=%async_computation | async-start | bytes 1179648 | tf_op jit(solution)/shard_map/while/body/eval_jaxpr/cond/branch_1_fun/all_to_all | solution.py:18
  460.3 4.0 copy-start.1
  470.0 15.1 %all-to-all-start.1 = ((bf16[2,8,9,17,128]{4,0,3,2,1:T(2,128)(2,1)}), bf16[2,8,9,17,128]{4,0,3,2,1:T(2,128)(2,1)S(1)}, u32[]{:S(2)}, u32[]{:S(2)}) async-start(bf16[2,8,9,17,128]{4,0,3,2,1:T(2,128)(2,1)} %copy.44), calls=%async_computation.1 | async-start | bytes 1253376 | tf_op jit(solution)/shard_map/while/body/eval_jaxpr/cond/branch_1_fun/all_to_all | solution.py:18
  486.1 2.5 copy-start.10
  (10 other events, 15.0 us)
